TPU v7x, 128 devices: a whole 4x4x4 slice. The times are simulated.
128 devices in a mesh: shard: 8 (over x, core), tensor: 16 (over z, y).
Axes of the slice: x: 4, y: 4, z: 4, core: 2. Of those that a mesh axis runs over, the one named last changes fastest.
Arguments:
- grad_square: bfloat16 [8, 768, 768], P(None, 'shard'), may hold values from -64 to 64
- grad_wide: bfloat16 [8, 2048, 768], P(None, 'shard'), may hold values from -64 to 64
- moment_square: float32 [8, 589824], P(None, ('shard', 'tensor')), may hold values from -6 to 6
- moment_wide: float32 [8, 1572864], P(None, ('shard', 'tensor')), may hold values from -6 to 6
Outputs:
- update_square: float32 [8, 768, 768], P(None, 'shard')
- update_wide: float32 [8, 2048, 768], P(None, 'shard')
- new_moment_square: float32 [8, 589824], P(None, ('shard', 'tensor'))
- new_moment_wide: float32 [8, 1572864], P(None, ('shard', 'tensor'))
All inputs are finite; a program needn't handle non-finite values.
Results may differ from a plain program's by a relative error of at most 0.0003.
Values sent between devices are 32-bit elements; how exact they have to be, the bound alone decides.
No kernel may reach another device: no remote copies, remote signals or barrier semaphores. Data moves between devices by JAX's collectives and lax.ppermute only.
A program may use at most 128 MiB of HBM per device.

v0:
```python
import math

import jax
import jax.numpy as jnp
from jax import lax
from jax.sharding import PartitionSpec as P

D = 768
FF = 2048
ITERS = 3


coef_a = 3.4445
coef_b = -4.775
coef_c = 2.0315
momentum_decay = 0.95
epsilon = 1e-07


def polynomial(row_gram, whole_gram):
    square_part = jnp.einsum(
        "mcd,mde->mce",
        row_gram,
        whole_gram,
        precision=lax.Precision.HIGHEST,
        preferred_element_type=jnp.float32,
    )
    return coef_b * row_gram + coef_c * square_part


def next_iterate(current, mixer):
    product = jnp.einsum(
        "mrc,mcd->mrd",
        current,
        mixer,
        precision=lax.Precision.HIGHEST,
        preferred_element_type=jnp.float32,
    )
    return coef_a * current + product


def partial_gram(current):
    return jnp.einsum(
        "mrc,mrd->mcd",
        current,
        current,
        precision=lax.Precision.HIGHEST,
        preferred_element_type=jnp.float32,
    )


def squares(values):
    return jnp.sum(values * values, axis=(1, 2))


def normalize(values, totals):
    return values / (jnp.sqrt(totals) + epsilon)[:, None, None]


def own_rows(grad, member, tensor_count):
    row_piece = grad.shape[1] // tensor_count
    return lax.dynamic_slice_in_dim(grad, member * row_piece, row_piece, 1)


def shards(grad_square, grad_wide, moment_square, moment_wide):
    tensor_count = lax.axis_size("tensor")
    member = lax.axis_index("tensor")
    flat_square = own_rows(grad_square, member, tensor_count).astype(jnp.float32)
    flat_wide = own_rows(grad_wide, member, tensor_count).astype(jnp.float32)
    new_square = momentum_decay * moment_square.reshape(flat_square.shape) + flat_square
    new_wide = momentum_decay * moment_wide.reshape(flat_wide.shape) + flat_wide
    look_square = flat_square + momentum_decay * new_square
    look_wide = flat_wide + momentum_decay * new_wide
    total_square, total_wide = lax.psum(
        (squares(look_square), squares(look_wide)), ("shard", "tensor")
    )
    start_square = normalize(look_square, total_square)
    start_wide = normalize(look_wide, total_wide)
    held_square, held_wide = (
        lax.all_to_all(start_square, "shard", split_axis=0, concat_axis=1, tiled=True),
        lax.all_to_all(start_wide, "shard", split_axis=0, concat_axis=1, tiled=True),
    )
    for iteration in range(ITERS):
        part_square = partial_gram(held_square)
        part_wide = partial_gram(held_wide)
        gram_square, gram_wide = lax.psum((part_square, part_wide), "tensor")
        mixer_square = polynomial(gram_square, gram_square)
        mixer_wide = polynomial(gram_wide, gram_wide)
        held_square = next_iterate(held_square, mixer_square)
        held_wide = next_iterate(held_wide, mixer_wide)
    scaled_square = math.sqrt(D) * held_square
    scaled_wide = math.sqrt(FF) * held_wide
    back_square, back_wide = (
        lax.all_to_all(scaled_square, "shard", split_axis=1, concat_axis=0, tiled=True),
        lax.all_to_all(scaled_wide, "shard", split_axis=1, concat_axis=0, tiled=True),
    )
    update_square, update_wide = (
        lax.all_gather(back_square, "tensor", axis=1, tiled=True),
        lax.all_gather(back_wide, "tensor", axis=1, tiled=True),
    )
    return (
        update_square,
        update_wide,
        new_square.reshape(moment_square.shape),
        new_wide.reshape(moment_wide.shape),
    )


def solution(mesh):
    return jax.shard_map(
        shards,
        mesh=mesh,
        in_specs=(
            P(None, "shard", None),
            P(None, "shard", None),
            P(None, ("shard", "tensor")),
            P(None, ("shard", "tensor")),
        ),
        out_specs=(
            P(None, "shard", None),
            P(None, "shard", None),
            P(None, ("shard", "tensor")),
            P(None, ("shard", "tensor")),
        ),
        check_vma=False,
    )
```

profile of v0, /device:TPU:1, one launch (start us, length us, event | category | flops | bytes accessed | tf_op | source)
XLA Modules:
  0.0 619.9 jit_solution(17534331259739057778)
XLA Ops:
  11.3 68.6 %all-reduce = (f32[8]{0:T(128)S(1)}, f32[8]{0:T(128)S(1)}) all-reduce(f32[8]{0:T(128)S(1)} %get-tuple-element.23, f32[8]{0:T(128)S(1)} %multiply_reduce_fusion), channel_id=1, replica_groups=mesh['shard'=8,'tensor'=16] {'shard','tensor'}, use_global_device_ids=true, to_apply=%region_1.0 | all-reduce | flops 16 | bytes 128 | tf_op jit(solution)/shard_map/psum | solution.py:74
  80.7 4.2 all-to-all-start
  84.9 2.0 fusion.78
  86.9 3.9 all-to-all-done
  90.8 4.3 all-to-all-start.2
  95.1 3.5 convolution_bitcast_fusion
  98.6 4.3 all-to-all-done.2
  102.9 3.5 convolution_bitcast_fusion.3
  106.6 105.0 %all-reduce.12.cloned.1.call-done = (f32[1,768,768]{2,1,0:T(8,128)}, f32[1,768,768]{2,1,0:T(8,128)}) async-done(((f32[1,768,768]{2,1,0:T(8,128)}, f32[1,768,768]{2,1,0:T(8,128)}), (f32[1,768,768]{2,1,0:T(8,128)}, f32[1,768,768]{2,1,0:T(8,128)})) %all-reduce.12.cloned.1.call-update) | async-done | bytes 4718608 | tf_op jit(solution)/shard_map/psum | solution.py:86
  211.6 8.5 %fusion.22 = f32[768,768]{1,0:T(8,128)S(1)} fusion(f32[1,768,768]{2,1,0:T(8,128)} %get-tuple-element.18), kind=kOutput, calls=%fused_computation.28 | convolution fusion | flops 5435817984 | bytes 4718592 | tf_op jit(solution)/shard_map/mcd,mde->mce/dot_general | solution.py:21
  220.1 1.8 fusion.63
  221.9 3.5 convolution_bitcast_fusion.5
  225.4 6.4 %fusion.10 = f32[768,768]{1,0:T(8,128)S(1)} fusion(f32[1,768,768]{2,1,0:T(8,128)S(1)} %copy-done.6), kind=kOutput, calls=%fused_computation.13 | convolution fusion | flops 5435817984 | bytes 4718592 | tf_op jit(solution)/shard_map/mcd,mde->mce/dot_general | solution.py:21
  233.4 3.5 convolution_bitcast_fusion.2
  237.0 108.1 %all-reduce.10.cloned.1.call-done = (f32[1,768,768]{2,1,0:T(8,128)}, f32[1,768,768]{2,1,0:T(8,128)}) async-done(((f32[1,768,768]{2,1,0:T(8,128)}, f32[1,768,768]{2,1,0:T(8,128)}), (f32[1,768,768]{2,1,0:T(8,128)}, f32[1,768,768]{2,1,0:T(8,128)})) %all-reduce.10.cloned.1.call-update) | async-done | bytes 4718608 | tf_op jit(solution)/shard_map/psum | solution.py:86
  345.1 8.5 %fusion.18 = f32[768,768]{1,0:T(8,128)S(1)} fusion(f32[1,768,768]{2,1,0:T(8,128)} %get-tuple-element.16), kind=kOutput, calls=%fused_computation.23 | convolution fusion | flops 5435817984 | bytes 4718592 | tf_op jit(solution)/shard_map/mcd,mde->mce/dot_general | solution.py:21
  353.6 1.8 fusion.66
  355.4 3.5 convolution_bitcast_fusion.4
  358.8 6.1 fusion.6
  365.0 1.7 fusion.39
  366.7 3.5 convolution_bitcast_fusion.1
  370.2 108.1 %all-reduce.8.cloned.1.call-done = (f32[1,768,768]{2,1,0:T(8,128)}, f32[1,768,768]{2,1,0:T(8,128)}) async-done(((f32[1,768,768]{2,1,0:T(8,128)}, f32[1,768,768]{2,1,0:T(8,128)}), (f32[1,768,768]{2,1,0:T(8,128)}, f32[1,768,768]{2,1,0:T(8,128)})) %all-reduce.8.cloned.1.call-update) | async-done | bytes 4718608 | tf_op jit(solution)/shard_map/psum | solution.py:86
  478.3 8.5 %fusion.14 = f32[768,768]{1,0:T(8,128)S(1)} fusion(f32[1,768,768]{2,1,0:T(8,128)} %get-tuple-element.14), kind=kOutput, calls=%fused_computation.18 | convolution fusion | flops 5435817984 | bytes 4718592 | tf_op jit(solution)/shard_map/mcd,mde->mce/dot_general | solution.py:21
  486.9 1.8 fusion.75
  488.8 10.3 %all_to_all.48 = f32[1,48,768]{2,0,1:T(1,128)S(1)} all-to-all(f32[1,48,768]{2,0,1:T(1,128)S(1)} %copy.19), channel_id=1, replica_groups=mesh['shard'=8,'tensor'=16] {'shard'}, dimensions={1} | all-to-all | bytes 294912 | tf_op jit(solution)/shard_map/all_to_all | solution.py:94
  500.5 6.0 fusion.2
  506.4 1.8 fusion.48
  508.6 11.3 %all_to_all.49 = f32[1,128,768]{2,0,1:T(1,128)S(1)} all-to-all(f32[1,128,768]{2,0,1:T(1,128)S(1)} %copy.21), channel_id=1, replica_groups=mesh['shard'=8,'tensor'=16] {'shard'}, dimensions={1} | all-to-all | bytes 786432 | tf_op jit(solution)/shard_map/all_to_all | solution.py:95
  521.7 21.0 %all-gather.3.cloned.1.call-done = f32[8,96,768]{2,0,1:T(8,128)} async-done(((f32[8,6,768]{2,0,1:T(8,128)}), f32[8,96,768]{2,0,1:T(8,128)}) %all-gather.3.cloned.1.call-update) | async-done | bytes 2359312 | tf_op jit(solution)/shard_map/all_gather | solution.py:98
  542.7 3.8 copy.22
  546.5 60.6 %all-gather.5.cloned.1.call-done = f32[8,256,768]{2,1,0:T(8,128)} async-done(((f32[8,16,768]{2,1,0:T(8,128)}), f32[8,256,768]{2,1,0:T(8,128)}) %all-gather.5.cloned.1.call-update) | async-done | bytes 6291472 | tf_op jit(solution)/shard_map/all_gather | solution.py:99
  607.1 6.0 copy.51
  (45 shorter events, 10.7 us)
Async XLA Ops:
  7.2 2.1 copy-start
  80.7 10.1 %all-to-all-start = ((f32[8,6,768]{2,1,0:T(8,128)}), f32[8,6,768]{2,1,0:T(8,128)S(1)}, u32[]{:S(2)}, u32[]{:S(2)}) async-start(f32[8,6,768]{2,1,0:T(8,128)} %copy.18), calls=%async_computation | async-start | bytes 393216 | tf_op jit(solution)/shard_map/all_to_all | solution.py:80
  90.8 12.0 %all-to-all-start.2 = ((f32[8,16,768]{2,1,0:T(8,128)}), f32[8,16,768]{2,1,0:T(8,128)S(1)}, u32[]{:S(2)}, u32[]{:S(2)}) async-start(f32[8,16,768]{2,1,0:T(8,128)} %get-tuple-element.21), calls=%async_computation.2 | async-start | bytes 786432 | tf_op jit(solution)/shard_map/all_to_all | solution.py:81
  95.1 116.4 %all-reduce.12.cloned.1.call-start = ((), (), s32[]{:S(2)}) async-start(), calls=%async_computation.8 | async-start | bytes 9437184 | tf_op jit(solution)/shard_map/psum | solution.py:86
  106.3 238.7 %all-reduce.10.cloned.1.call-start = ((), (), s32[]{:S(2)}) async-start(), calls=%async_computation.7 | async-start | bytes 9437184 | tf_op jit(solution)/shard_map/psum | solution.py:86
  211.6 8.5 %copy-start.2 = (f32[1,768,768]{2,1,0:T(8,128)S(1)}, f32[1,768,768]{2,1,0:T(8,128)}, u32[]{:S(2)}) copy-start(f32[1,768,768]{2,1,0:T(8,128)} %get-tuple-element.18) | copy-start | bytes 7077892
  221.9 3.5 copy-start.6
  236.9 241.4 %all-reduce.8.cloned.1.call-start = ((), (), s32[]{:S(2)}) async-start(), calls=%async_computation.6 | async-start | bytes 9437184 | tf_op jit(solution)/shard_map/psum | solution.py:86
  345.1 8.5 %copy-start.3 = (f32[1,768,768]{2,1,0:T(8,128)S(1)}, f32[1,768,768]{2,1,0:T(8,128)}, u32[]{:S(2)}) copy-start(f32[1,768,768]{2,1,0:T(8,128)} %get-tuple-element.16) | copy-start | bytes 7077892
  355.4 3.5 copy-start.7
  370.2 172.5 %all-gather.3.cloned.1.call-start = ((), (), s32[]{:S(2)}) async-start(), calls=%async_computation.4 | async-start | bytes 2506752 | tf_op jit(solution)/shard_map/all_gather | solution.py:98
  478.3 8.5 %copy-start.4 = (f32[1,768,768]{2,1,0:T(8,128)S(1)}, f32[1,768,768]{2,1,0:T(8,128)}, u32[]{:S(2)}) copy-start(f32[1,768,768]{2,1,0:T(8,128)} %get-tuple-element.14) | copy-start | bytes 7077892
  486.9 13.6 %copy-start.5 = (f32[1,768,768]{2,1,0:T(8,128)S(1)}, f32[1,768,768]{2,1,0:T(8,128)}, u32[]{:S(2)}) copy-start(f32[1,768,768]{2,1,0:T(8,128)} %get-tuple-element.15) | copy-start | bytes 7077892
  500.2 106.9 %all-gather.5.cloned.1.call-start = ((), (), s32[]{:S(2)}) async-start(), calls=%async_computation.5 | async-start | bytes 6684672 | tf_op jit(solution)/shard_map/all_gather | solution.py:99
  508.2 12.5 %copy-start.8 = (f32[1,8,16,768]{3,2,1,0:T(8,128)S(1)}, f32[1,8,16,768]{3,2,1,0:T(8,128)}, u32[]{:S(2)}) copy-start(f32[1,8,16,768]{3,2,1,0:T(8,128)} %get-tuple-element.20) | copy-start | bytes 1179652
  607.1 6.0 copy-start.1
Sparse Core Ops, SparseCore 0:
  106.5 105.0 all-reduce.11
  237.0 107.9 all-reduce.9
  370.3 107.9 all-reduce.7
  500.3 42.3 all-gather.2
  545.3 61.8 all-gather.4
where the time goes:
time: 625 us; the launch traced here: 620 us
  waiting for transfers between devices  411 us (66%)
  blocking collectives  90.2 us (14%)
  matrix products  75.2 us (12%)
  between operations  14.3 us (2%)
  local copies, waits for them, and re-layouts  13.7 us (2%)
  starting transfers between devices  9.07 us (1%)
  other arithmetic  6.42 us (1%)
    psum x3, waiting for transfers between devices, shards(): gram_square, gram_wide = lax.psum((part_square, part_wide), 'tensor')  321 us
    psum x1, blocking collectives, shards(): lax.psum((squares(look_square), squares(look_wide)), ('shard', 'tensor'))  68.6 us
    all_gather x1, waiting for transfers between devices, shards(): lax.all_gather(back_wide, 'tensor', axis=1, tiled=True)  60.6 us
    dot_general x6, matrix products, polynomial(): jnp.einsum('mcd,mde->mce', row_gram, whole_gram, precision=lax.Precision....  44 us
    all_gather x1, waiting for transfers between devices, shards(): lax.all_gather(back_square, 'tensor', axis=1, tiled=True)  21 us
    dot_general x6, matrix products, partial_gram(): jnp.einsum('mrc,mrd->mcd', current, current, precision=lax.Precision.HIGH...  20.8 us
  transfers between devices with their start and end apart: 7, of which 7 were waited for; matrix products, arithmetic and copies ran while one was open for 3% of the time, Pallas kernels for 0%

commit v1 on v0

v1 whole, which is shorter than its diff:
```python
import math

import jax
import jax.numpy as jnp
from jax import lax
from jax.sharding import PartitionSpec as P

D = 768
FF = 2048
ITERS = 3


coef_a = 3.4445
coef_b = -4.775
coef_c = 2.0315
momentum_decay = 0.95
epsilon = 1e-07

HIGHEST = lax.Precision.HIGHEST


def dot(x, y):
    return jnp.dot(x, y, precision=HIGHEST, preferred_element_type=jnp.float32)


def gram_of(rows):
    return lax.dot_general(
        rows,
        rows,
        (((0,), (0,)), ((), ())),
        precision=HIGHEST,
        preferred_element_type=jnp.float32,
    )


def own_rows(grad, member, tensor_count):
    row_piece = grad.shape[1] // tensor_count
    return lax.dynamic_slice_in_dim(grad, member * row_piece, row_piece, 1)


def shards(grad_square, grad_wide, moment_square, moment_wide):
    tensor_count = lax.axis_size("tensor")
    member = lax.axis_index("tensor")
    count_square, count_wide = grad_square.shape[0], grad_wide.shape[0]
    assert count_square == count_wide and 2 * count_square == tensor_count
    flat_square = own_rows(grad_square, member, tensor_count).astype(jnp.float32)
    flat_wide = own_rows(grad_wide, member, tensor_count).astype(jnp.float32)
    new_square = momentum_decay * moment_square.reshape(flat_square.shape) + flat_square
    new_wide = momentum_decay * moment_wide.reshape(flat_wide.shape) + flat_wide
    look_square = flat_square + momentum_decay * new_square
    look_wide = flat_wide + momentum_decay * new_wide

    piece = look_wide.shape[1]
    pad = piece - look_square.shape[1]
    padded_square = jnp.pad(look_square, ((0, 0), (0, pad), (0, 0)))
    send = jnp.stack([padded_square, look_wide], axis=1).reshape(
        tensor_count, piece, look_wide.shape[2]
    )
    held = lax.all_to_all(send, "tensor", split_axis=0, concat_axis=0, tiled=True)
    rows = held.reshape(tensor_count * piece, held.shape[2])

    gram = lax.psum(gram_of(rows), "shard")
    columns = gram.shape[0]
    eye = jnp.eye(columns, dtype=jnp.float32)
    total = jnp.sum(gram * eye)
    denom = jnp.sqrt(total) + epsilon
    current = rows / denom
    gram = gram / (denom * denom)
    for iteration in range(ITERS):
        square_gram = dot(gram, gram)
        mixer = coef_b * gram + coef_c * square_gram
        current = coef_a * current + dot(current, mixer)
        if iteration + 1 < ITERS:
            full = mixer + coef_a * eye
            gram = dot(full, dot(gram, full))

    is_square = member % 2 == 0
    scale = jnp.where(
        is_square, jnp.float32(math.sqrt(D)), jnp.float32(math.sqrt(FF))
    )
    update = scale * current
    gathered = lax.all_gather(update[None], "tensor", axis=0, tiled=True)
    gathered = gathered.reshape(count_square, 2, tensor_count, piece, update.shape[1])
    update_square = gathered[:, 0, :, : piece - pad].reshape(
        count_square, tensor_count * (piece - pad), update.shape[1]
    )
    update_wide = gathered[:, 1].reshape(
        count_wide, tensor_count * piece, update.shape[1]
    )
    return (
        update_square,
        update_wide,
        new_square.reshape(moment_square.shape),
        new_wide.reshape(moment_wide.shape),
    )


def solution(mesh):
    return jax.shard_map(
        shards,
        mesh=mesh,
        in_specs=(
            P(None, "shard", None),
            P(None, "shard", None),
            P(None, ("shard", "tensor")),
            P(None, ("shard", "tensor")),
        ),
        out_specs=(
            P(None, "shard", None),
            P(None, "shard", None),
            P(None, ("shard", "tensor")),
            P(None, ("shard", "tensor")),
        ),
        check_vma=False,
    )
```

time: 625 us -> 278 us (0.44)
  waiting for transfers between devices: 411 us -> 155 us
  blocking collectives: 90.2 us -> 21.9 us
  matrix products: 75.2 us -> 58.1 us
  starting transfers between devices: 9.07 us -> 0.08 us
    psum x3 -> x1, waiting for transfers between devices: 321 us -> 63.2 us  [shards(): gram = lax.psum(gram_of(rows), 'shard')]
    psum x1 -> x0, blocking collectives: 68.6 us -> none  [shards(): lax.psum((squares(look_square), squares(look_wide)), ('shard', 'tensor'))]
    dot_general x18 -> x11, matrix products: 75.2 us -> 58.1 us  [the longest x10 54.6 us: dot(): return jnp.dot(x, y, precision=HIGHEST, preferred_element_type=jnp.float32)]
    all_gather x2 -> x1, waiting for transfers between devices: 81.5 us -> 91.5 us  [shards(): gathered = lax.all_gather(update[None], 'tensor', axis=0, tiled=True)]
    all_to_all x2 -> x0, starting transfers between devices: 8.51 us -> none  [the longest x1 4.31 us: shards(): lax.all_to_all(start_wide, 'shard', split_axis=0, concat_axis=1, tiled=True)]
    all_to_all x2 -> x0, waiting for transfers between devices: 8.17 us -> none  [the longest x1 4.25 us: shards(): lax.all_to_all(start_wide, 'shard', split_axis=0, concat_axis=1, tiled=True)]
    slice x0 -> x2, local copies, waits for them, and re-layouts: none -> 8.12 us  [the longest x1 5.94 us: shards(): gathered[:, 1].reshape(count_wide, tensor_count * piece, update.shape[1])]
    unnamed x22 -> x10, local copies, waits for them, and re-layouts: 11.7 us -> 4.39 us
  transfers between devices with their start and end apart: 7 -> 2, of which waited for: 7 -> 2; matrix products, arithmetic and copies ran while one was open for 3% -> 0% of each run, Pallas kernels for 0% -> 0%
where the time goes in v1:
time: 278 us; the launch traced here: 273 us
  waiting for transfers between devices  155 us (56%)
  matrix products  58.1 us (21%)
  blocking collectives  21.9 us (8%)
  between operations  15.3 us (6%)
  local copies, waits for them, and re-layouts  14.5 us (5%)
  other arithmetic  8.74 us (3%)
    all_gather x1, waiting for transfers between devices, shards(): gathered = lax.all_gather(update[None], 'tensor', axis=0, tiled=True)  91.5 us
    psum x1, waiting for transfers between devices, shards(): gram = lax.psum(gram_of(rows), 'shard')  63.2 us
    dot_general x10, matrix products, dot(): return jnp.dot(x, y, precision=HIGHEST, preferred_element_type=jnp.float32)  54.6 us
    all_to_all x1, blocking collectives, shards(): lax.all_to_all(send, 'tensor', split_axis=0, concat_axis=0, tiled=True)  21.9 us
    slice x1, local copies, waits for them, and re-layouts, shards(): gathered[:, 1].reshape(count_wide, tensor_count * piece, update.shape[1])  5.94 us
  transfers between devices with their start and end apart: 2, of which 2 were waited for; matrix products, arithmetic and copies ran while one was open for 0% of the time, Pallas kernels for 0%

profile of v1, /device:TPU:1, one launch (start us, length us, event | category | flops | bytes accessed | tf_op | source)
XLA Modules:
  0.0 273.4 jit_solution(14698647721890941587)
XLA Ops:
  7.2 0.0 all-reduce.3.cloned.1.call-start
  7.2 1.2 broadcast_multiply_fusion
  8.4 1.6 broadcast_multiply_fusion.1
  10.0 1.0 constant_dynamic-slice_fusion.1
  11.0 1.6 convert_add_fusion.3
  12.6 0.8 pad_bitcast_fusion
  13.4 0.9 convert_add_fusion.1
  14.2 1.0 pad_maximum_fusion
  15.3 0.3 copy.13
  15.5 21.9 %all_to_all.5 = f32[16,16,768]{2,1,0:T(8,128)S(1)} all-to-all(f32[16,16,768]{2,1,0:T(8,128)S(1)} %bitcast.33), channel_id=1, replica_groups=mesh['shard'=8,'tensor'=16] {'tensor'}, dimensions={0} | all-to-all | bytes 1572864 | tf_op jit(solution)/shard_map/all_to_all | solution.py:59
  37.5 0.9 copy-done.1
  38.3 3.5 %convolution_bitcast_fusion = f32[768,768]{1,0:T(8,128)} fusion(f32[16,16,768]{2,1,0:T(8,128)S(1)} %all_to_all.5), kind=kOutput, calls=%fused_computation.14 | convolution fusion | flops 1811939328 | bytes 3145728 | tf_op jit(solution)/shard_map/dot_general | solution.py:27
  41.8 0.0 all-reduce.3.cloned.1.call-update
  41.8 0.0 all-gather.3.cloned.1.call-start
  41.9 63.2 %all-reduce.3.cloned.1.call-done = f32[768,768]{1,0:T(8,128)} async-done(((f32[768,768]{1,0:T(8,128)}), f32[768,768]{1,0:T(8,128)}) %all-reduce.3.cloned.1.call-update) | async-done | bytes 2359312 | tf_op jit(solution)/shard_map/psum | solution.py:62
  105.1 2.4 select_reduce_fusion
  108.2 10.1 %multiply_add_fusion.1 = f32[768,768]{1,0:T(8,128)S(1)} fusion(f32[768,768]{1,0:T(8,128)} %all-reduce.3.cloned.1.call-done, f32[]{:T(128)S(6)} %mul.80), kind=kOutput, calls=%fused_computation.7 | convolution fusion | flops 5438767104 | bytes 4718596 | tf_op jit(solution)/shard_map/dot_general | solution.py:23
  118.3 6.0 %fusion.5 = f32[768,768]{1,0:T(8,128)S(1)} fusion(f32[768,768]{1,0:T(8,128)S(1)} %multiply_add_fusion.1, f32[768,768]{1,0:T(8,128)S(1)} %copy-done.3, f32[]{:T(128)S(6)} %mul.80), kind=kOutput, calls=%fused_computation.11 | convolution fusion | flops 5438177280 | bytes 7077892 | tf_op jit(solution)/shard_map/dot_general | solution.py:23
  124.3 6.0 %fusion.4 = f32[768,768]{1,0:T(8,128)S(1)} fusion(f32[768,768]{1,0:T(8,128)S(1)} %fusion.5, f32[768,768]{1,0:T(8,128)S(1)} %multiply_add_fusion.1), kind=kOutput, calls=%fused_computation.10 | convolution fusion | flops 5437587456 | bytes 7077888 | tf_op jit(solution)/shard_map/dot_general | solution.py:23
  130.3 6.3 %multiply_add_fusion = f32[768,768]{1,0:T(8,128)S(1)} fusion(f32[768,768]{1,0:T(8,128)S(1)} %fusion.4), kind=kOutput, calls=%fused_computation.6 | convolution fusion | flops 5437587456 | bytes 4718592 | tf_op jit(solution)/shard_map/dot_general | solution.py:23
  136.6 6.0 %fusion.7 = f32[768,768]{1,0:T(8,128)S(1)} fusion(f32[768,768]{1,0:T(8,128)S(1)} %fusion.4, f32[768,768]{1,0:T(8,128)S(1)} %multiply_add_fusion), kind=kOutput, calls=%fused_computation.13 | convolution fusion | flops 5437587456 | bytes 7077888 | tf_op jit(solution)/shard_map/dot_general | solution.py:23
  142.6 6.2 %fusion.6 = f32[768,768]{1,0:T(8,128)S(1)} fusion(f32[768,768]{1,0:T(8,128)S(1)} %fusion.7, f32[768,768]{1,0:T(8,128)S(1)} %multiply_add_fusion), kind=kOutput, calls=%fused_computation.12 | convolution fusion | flops 5437587456 | bytes 7077888 | tf_op jit(solution)/shard_map/dot_general | solution.py:23
  148.8 6.0 %fusion.35 = f32[768,768]{1,0:T(8,128)S(1)} fusion(f32[768,768]{1,0:T(8,128)S(1)} %fusion.6), kind=kOutput, calls=%fused_computation.52 | convolution fusion | flops 5435817984 | bytes 4718592 | tf_op jit(solution)/shard_map/dot_general | solution.py:23
  154.8 0.1 broadcast_divide_fusion.3
  154.9 2.3 convolution_add_fusion.1
  157.2 2.5 convolution_add_fusion
  159.7 3.3 %fusion.11 = f32[256,768]{1,0:T(8,128)} fusion(f32[256,768]{1,0:T(8,128)S(1)} %convolution_add_fusion, f32[768,768]{1,0:T(8,128)S(1)} %fusion.35, f32[768,768]{1,0:T(8,128)S(1)} %fusion.6, f32[]{:T(128)S(6)} %select_n.18), kind=kOutput, calls=%fused_computation.18 | convolution fusion | flops 1814298624 | bytes 6291460 | tf_op jit(solution)/shard_map/dot_general | solution.py:23
  163.0 91.5 %all-gather.3.cloned.1.call-done = f32[4096,768]{1,0:T(8,128)} async-done(((f32[256,768]{1,0:T(8,128)}), f32[4096,768]{1,0:T(8,128)}) %all-gather.3.cloned.1.call-update) | async-done | bytes 12582928 | tf_op jit(solution)/shard_map/all_gather | solution.py:82
  254.5 2.2 slice.8
  256.7 5.9 %slice.9 = f32[8,1,16,16,768]{4,3,2,1,0:T(8,128)} slice(f32[8,2,16,16,768]{4,3,2,1,0:T(8,128)} %bitcast.31), slice={[0:8], [1:2], [0:16], [0:16], [0:768]} | slice | bytes 12582912 | tf_op jit(solution)/shard_map/slice | solution.py:87
  262.6 1.4 copy.18
  264.0 2.1 copy.15
  (9 shorter events, 0.1 us)
Async XLA Ops:
  7.2 6.2 %copy-start = (bf16[8,256,768]{2,1,0:T(8,128)(2,1)S(1)}, bf16[8,256,768]{2,1,0:T(8,128)(2,1)}, u32[]{:S(2)}) copy-start(bf16[8,256,768]{2,1,0:T(8,128)(2,1)} %param.5) | copy-start | bytes 9437188
  7.2 97.9 %all-reduce.3.cloned.1.call-start = ((), (), s32[]{:S(2)}) async-start(), calls=%async_computation.1 | async-start | bytes 4718592 | tf_op jit(solution)/shard_map/psum | solution.py:62
  37.5 0.9 copy-start.1
  41.8 212.7 %all-gather.3.cloned.1.call-start = ((), (), s32[]{:S(2)}) async-start(), calls=%async_computation.2 | async-start | bytes 13369344 | tf_op jit(solution)/shard_map/all_gather | solution.py:82
  108.2 10.1 %copy-start.3 = (f32[768,768]{1,0:T(8,128)S(1)}, f32[768,768]{1,0:T(8,128)}, u32[]{:S(2)}) copy-start(f32[768,768]{1,0:T(8,128)} %all-reduce.3.cloned.1.call-done) | copy-start | bytes 7077892
  148.8 6.0 %copy-start.2 = (f32[16,16,768]{2,1,0:T(8,128)S(1)}, f32[16,16,768]{2,1,0:T(8,128)}, u32[]{:S(2)}) copy-start(f32[16,16,768]{2,1,0:T(8,128)} %copy-done.1) | copy-start | bytes 2359300
Sparse Core Ops, SparseCore 0:
  41.9 63.1 all-reduce.2
  163.2 91.2 all-gather.2

commit v2 on v1

--- a/solution.py
+++ b/solution.py
@@ -16,11 +16,11 @@
 momentum_decay = 0.95
 epsilon = 1e-07
 
-HIGHEST = lax.Precision.HIGHEST
+PRECISION = lax.Precision.HIGH
 
 
 def dot(x, y):
-    return jnp.dot(x, y, precision=HIGHEST, preferred_element_type=jnp.float32)
+    return jnp.dot(x, y, precision=PRECISION, preferred_element_type=jnp.float32)
 
 
 def gram_of(rows):
@@ -28,7 +28,7 @@
         rows,
         rows,
         (((0,), (0,)), ((), ())),
-        precision=HIGHEST,
+        precision=PRECISION,
         preferred_element_type=jnp.float32,
     )
 

time: 278 us -> 249 us (0.90); the launches traced: 273 us -> 249 us
  matrix products: 58.1 us -> 33.7 us
    dot_general x11, matrix products: 58.1 us -> 33.7 us  [the longest x10 31 us: dot(): jnp.dot(x, y, precision=PRECISION, preferred_element_type=jnp.float32)]
where the time goes in v2:
time: 249 us
  waiting for transfers between devices  155 us (62%)
  matrix products  33.7 us (14%)
  blocking collectives  21.9 us (9%)
  between operations  14.9 us (6%)
  local copies, waits for them, and re-layouts  14.5 us (6%)
  other arithmetic  8.74 us (4%)
    all_gather x1, waiting for transfers between devices, shards(): gathered = lax.all_gather(update[None], 'tensor', axis=0, tiled=True)  91.5 us
    psum x1, waiting for transfers between devices, shards(): gram = lax.psum(gram_of(rows), 'shard')  63.1 us
    dot_general x10, matrix products, dot(): jnp.dot(x, y, precision=PRECISION, preferred_element_type=jnp.float32)  31 us
    all_to_all x1, blocking collectives, shards(): lax.all_to_all(send, 'tensor', split_axis=0, concat_axis=0, tiled=True)  21.9 us
    slice x1, local copies, waits for them, and re-layouts, shards(): gathered[:, 1].reshape(count_wide, tensor_count * piece, update.shape[1])  5.94 us
  transfers between devices with their start and end apart: 2, of which 2 were waited for; matrix products, arithmetic and copies ran while one was open for 0% of the time, Pallas kernels for 0%

profile of v2, /device:TPU:1, one launch (start us, length us, event | category | flops | bytes accessed | tf_op | source)
XLA Modules:
  0.0 248.6 jit_solution(4695802608199170934)
XLA Ops:
  7.2 0.0 all-reduce.3.cloned.1.call-start
  7.2 1.2 broadcast_multiply_fusion
  8.4 1.6 broadcast_multiply_fusion.1
  10.0 1.0 constant_dynamic-slice_fusion.1
  11.0 1.6 convert_add_fusion.3
  12.6 0.8 pad_bitcast_fusion
  13.4 0.9 convert_add_fusion.1
  14.2 1.0 pad_maximum_fusion
  15.3 0.3 copy.13
  15.5 21.9 %all_to_all.5 = f32[16,16,768]{2,1,0:T(8,128)S(1)} all-to-all(f32[16,16,768]{2,1,0:T(8,128)S(1)} %bitcast.33), channel_id=1, replica_groups=mesh['shard'=8,'tensor'=16] {'tensor'}, dimensions={0} | all-to-all | bytes 1572864 | tf_op jit(solution)/shard_map/all_to_all | solution.py:59
  37.5 0.9 copy-done.1
  38.3 2.7 %convolution_bitcast_fusion = f32[768,768]{1,0:T(8,128)} fusion(f32[16,16,768]{2,1,0:T(8,128)S(1)} %all_to_all.5), kind=kOutput, calls=%fused_computation.14 | convolution fusion | flops 905969664 | bytes 3145728 | tf_op jit(solution)/shard_map/dot_general | solution.py:27
  41.0 0.0 all-reduce.3.cloned.1.call-update
  41.0 0.2 all-gather.3.cloned.1.call-start
  41.3 63.1 %all-reduce.3.cloned.1.call-done = f32[768,768]{1,0:T(8,128)} async-done(((f32[768,768]{1,0:T(8,128)}), f32[768,768]{1,0:T(8,128)}) %all-reduce.3.cloned.1.call-update) | async-done | bytes 2359312 | tf_op jit(solution)/shard_map/psum | solution.py:62
  104.3 2.4 select_reduce_fusion
  107.4 6.4 %multiply_add_fusion.1 = f32[768,768]{1,0:T(8,128)S(1)} fusion(f32[768,768]{1,0:T(8,128)} %all-reduce.3.cloned.1.call-done, f32[]{:T(128)S(6)} %mul.80), kind=kOutput, calls=%fused_computation.7 | convolution fusion | flops 2720858112 | bytes 4718596 | tf_op jit(solution)/shard_map/dot_general | solution.py:23
  113.9 3.2 %fusion.5 = f32[768,768]{1,0:T(8,128)S(1)} fusion(f32[768,768]{1,0:T(8,128)S(1)} %multiply_add_fusion.1, f32[768,768]{1,0:T(8,128)S(1)} %copy-done.3, f32[]{:T(128)S(6)} %mul.80), kind=kOutput, calls=%fused_computation.11 | convolution fusion | flops 2720268288 | bytes 7077892 | tf_op jit(solution)/shard_map/dot_general | solution.py:23
  117.0 3.2 %fusion.4 = f32[768,768]{1,0:T(8,128)S(1)} fusion(f32[768,768]{1,0:T(8,128)S(1)} %fusion.5, f32[768,768]{1,0:T(8,128)S(1)} %multiply_add_fusion.1), kind=kOutput, calls=%fused_computation.10 | convolution fusion | flops 2719678464 | bytes 7077888 | tf_op jit(solution)/shard_map/dot_general | solution.py:23
  120.2 3.5 %multiply_add_fusion = f32[768,768]{1,0:T(8,128)S(1)} fusion(f32[768,768]{1,0:T(8,128)S(1)} %fusion.4), kind=kOutput, calls=%fused_computation.6 | convolution fusion | flops 2719678464 | bytes 4718592 | tf_op jit(solution)/shard_map/dot_general | solution.py:23
  123.7 3.1 %fusion.7 = f32[768,768]{1,0:T(8,128)S(1)} fusion(f32[768,768]{1,0:T(8,128)S(1)} %fusion.4, f32[768,768]{1,0:T(8,128)S(1)} %multiply_add_fusion), kind=kOutput, calls=%fused_computation.13 | convolution fusion | flops 2719678464 | bytes 7077888 | tf_op jit(solution)/shard_map/dot_general | solution.py:23
  126.9 3.2 %fusion.6 = f32[768,768]{1,0:T(8,128)S(1)} fusion(f32[768,768]{1,0:T(8,128)S(1)} %fusion.7, f32[768,768]{1,0:T(8,128)S(1)} %multiply_add_fusion), kind=kOutput, calls=%fused_computation.12 | convolution fusion | flops 2719678464 | bytes 7077888 | tf_op jit(solution)/shard_map/dot_general | solution.py:23
  130.1 3.1 %fusion.35 = f32[768,768]{1,0:T(8,128)S(1)} fusion(f32[768,768]{1,0:T(8,128)S(1)} %fusion.6), kind=kOutput, calls=%fused_computation.52 | convolution fusion | flops 2717908992 | bytes 4718592 | tf_op jit(solution)/shard_map/dot_general | solution.py:23
  133.2 0.1 broadcast_divide_fusion.3
  133.3 1.4 convolution_add_fusion.1
  134.7 1.4 convolution_add_fusion
  136.1 2.5 %fusion.11 = f32[256,768]{1,0:T(8,128)} fusion(f32[256,768]{1,0:T(8,128)S(1)} %convolution_add_fusion, f32[768,768]{1,0:T(8,128)S(1)} %fusion.35, f32[768,768]{1,0:T(8,128)S(1)} %fusion.6, f32[]{:T(128)S(6)} %select_n.18), kind=kOutput, calls=%fused_computation.18 | convolution fusion | flops 908328960 | bytes 6291460 | tf_op jit(solution)/shard_map/dot_general | solution.py:23
  138.7 91.5 %all-gather.3.cloned.1.call-done = f32[4096,768]{1,0:T(8,128)} async-done(((f32[256,768]{1,0:T(8,128)}), f32[4096,768]{1,0:T(8,128)}) %all-gather.3.cloned.1.call-update) | async-done | bytes 12582928 | tf_op jit(solution)/shard_map/all_gather | solution.py:82
  230.1 2.2 slice.8
  232.3 5.9 %slice.9 = f32[8,1,16,16,768]{4,3,2,1,0:T(8,128)} slice(f32[8,2,16,16,768]{4,3,2,1,0:T(8,128)} %bitcast.31), slice={[0:8], [1:2], [0:16], [0:16], [0:768]} | slice | bytes 12582912 | tf_op jit(solution)/shard_map/slice | solution.py:87
  238.3 1.4 copy.18
  239.6 2.1 copy.15
  (9 shorter events, 0.1 us)
Async XLA Ops:
  7.2 6.2 %copy-start = (bf16[8,256,768]{2,1,0:T(8,128)(2,1)S(1)}, bf16[8,256,768]{2,1,0:T(8,128)(2,1)}, u32[]{:S(2)}) copy-start(bf16[8,256,768]{2,1,0:T(8,128)(2,1)} %param.5) | copy-start | bytes 9437188
  7.2 97.2 %all-reduce.3.cloned.1.call-start = ((), (), s32[]{:S(2)}) async-start(), calls=%async_computation.1 | async-start | bytes 4718592 | tf_op jit(solution)/shard_map/psum | solution.py:62
  37.5 0.9 copy-start.1
  41.0 189.1 %all-gather.3.cloned.1.call-start = ((), (), s32[]{:S(2)}) async-start(), calls=%async_computation.2 | async-start | bytes 13369344 | tf_op jit(solution)/shard_map/all_gather | solution.py:82
  107.4 6.5 %copy-start.3 = (f32[768,768]{1,0:T(8,128)S(1)}, f32[768,768]{1,0:T(8,128)}, u32[]{:S(2)}) copy-start(f32[768,768]{1,0:T(8,128)} %all-reduce.3.cloned.1.call-done) | copy-start | bytes 7077892
  130.0 3.2 %copy-start.2 = (f32[16,16,768]{2,1,0:T(8,128)S(1)}, f32[16,16,768]{2,1,0:T(8,128)}, u32[]{:S(2)}) copy-start(f32[16,16,768]{2,1,0:T(8,128)} %copy-done.1) | copy-start | bytes 2359300
Sparse Core Ops, SparseCore 0:
  41.2 63.1 all-reduce.2
  138.8 91.2 all-gather.2

commit v3 on v2

--- a/solution.py
+++ b/solution.py
@@ -79,14 +79,22 @@
         is_square, jnp.float32(math.sqrt(D)), jnp.float32(math.sqrt(FF))
     )
     update = scale * current
-    gathered = lax.all_gather(update[None], "tensor", axis=0, tiled=True)
-    gathered = gathered.reshape(count_square, 2, tensor_count, piece, update.shape[1])
-    update_square = gathered[:, 0, :, : piece - pad].reshape(
-        count_square, tensor_count * (piece - pad), update.shape[1]
-    )
-    update_wide = gathered[:, 1].reshape(
-        count_wide, tensor_count * piece, update.shape[1]
-    )
+    square_piece = piece - pad
+    square_rows = update.reshape(tensor_count, piece, -1)[:, :square_piece]
+    square_rows = square_rows.reshape(tensor_count * square_piece, -1)
+    square_half = square_rows.shape[0] // 2
+    wide_half = update.shape[0] // 2
+    pairs = count_square
+    to_odd = [(2 * j, 2 * j + 1) for j in range(pairs)]
+    to_even = [(2 * j + 1, 2 * j) for j in range(pairs)]
+    got_square = lax.ppermute(square_rows[square_half:], "tensor", to_odd)
+    got_wide = lax.ppermute(update[:wide_half], "tensor", to_even)
+    mine_square = jnp.where(is_square, square_rows[:square_half], got_square)
+    mine_wide = jnp.where(is_square, got_wide, update[wide_half:])
+    update_square = lax.all_gather(mine_square, "tensor", axis=0, tiled=True)
+    update_wide = lax.all_gather(mine_wide, "tensor", axis=0, tiled=True)
+    update_square = update_square.reshape(count_square, -1, update.shape[1])
+    update_wide = update_wide.reshape(count_wide, -1, update.shape[1])
     return (
         update_square,
         update_wide,

time: 249 us -> 274 us (1.10)
  waiting for transfers between devices: 155 us -> 174 us
  starting transfers between devices: 0.26 us -> 5.36 us
    ppermute x0 -> x2, waiting for transfers between devices: none -> 10.3 us  [the longest x1 8.59 us: shards(): got_wide = lax.ppermute(update[:wide_half], 'tensor', to_even)]
    all_gather x1 -> x2, waiting for transfers between devices: 91.5 us -> 100 us  [the longest x1 64.6 us: shards(): update_wide = lax.all_gather(mine_wide, 'tensor', axis=0, tiled=True)]
    unnamed x10 -> x12, local copies, waits for them, and re-layouts: 4.39 us -> 10.9 us
    slice x2 -> x4, local copies, waits for them, and re-layouts: 8.12 us -> 1.76 us  [the longest x1 1.02 us: shards(): got_wide = lax.ppermute(update[:wide_half], 'tensor', to_even)]
    ppermute x0 -> x2, starting transfers between devices: none -> 5.06 us  [the longest x1 3.76 us: shards(): got_square = lax.ppermute(square_rows[square_half:], 'tensor', to_odd)]
  transfers between devices with their start and end apart: 2 -> 5, of which waited for: 2 -> 5; matrix products, arithmetic and copies ran while one was open for 0% -> 1% of each run, Pallas kernels for 0% -> 0%
where the time goes in v3:
time: 274 us
  waiting for transfers between devices  174 us (64%)
  matrix products  32.6 us (12%)
  blocking collectives  21.9 us (8%)
  local copies, waits for them, and re-layouts  14.7 us (5%)
  between operations  14.6 us (5%)
  other arithmetic  11.2 us (4%)
  starting transfers between devices  5.36 us (2%)
    all_gather x1, waiting for transfers between devices, shards(): update_wide = lax.all_gather(mine_wide, 'tensor', axis=0, tiled=True)  64.6 us
    psum x1, waiting for transfers between devices, shards(): gram = lax.psum(gram_of(rows), 'shard')  63.1 us
    all_gather x1, waiting for transfers between devices, shards(): update_square = lax.all_gather(mine_square, 'tensor', axis=0, tiled=True)  35.6 us
    dot_general x10, matrix products, dot(): jnp.dot(x, y, precision=PRECISION, preferred_element_type=jnp.float32)  29.9 us
    all_to_all x1, blocking collectives, shards(): lax.all_to_all(send, 'tensor', split_axis=0, concat_axis=0, tiled=True)  21.9 us
    unnamed x12, local copies, waits for them, and re-layouts  10.9 us
    ppermute x1, waiting for transfers between devices, shards(): got_wide = lax.ppermute(update[:wide_half], 'tensor', to_even)  8.59 us
  transfers between devices with their start and end apart: 5, of which 5 were waited for; matrix products, arithmetic and copies ran while one was open for 1% of the time, Pallas kernels for 0%

profile of v3, /device:TPU:1, one launch (start us, length us, event | category | flops | bytes accessed | tf_op | source)
XLA Modules:
  0.0 274.0 jit_solution(4553869851448595243)
XLA Ops:
  7.2 1.2 broadcast_multiply_fusion
  8.4 1.6 broadcast_multiply_fusion.1
  10.0 1.0 constant_dynamic-slice_fusion.1
  11.0 1.6 convert_add_fusion.3
  13.4 0.9 convert_add_fusion.1
  14.2 1.0 pad_maximum_fusion
  15.5 21.9 %all_to_all.5 = f32[16,16,768]{2,1,0:T(8,128)S(1)} all-to-all(f32[16,16,768]{2,1,0:T(8,128)S(1)} %bitcast.31), channel_id=1, replica_groups=mesh['shard'=8,'tensor'=16] {'tensor'}, dimensions={0} | all-to-all | bytes 1572864 | tf_op jit(solution)/shard_map/all_to_all | solution.py:59
  37.5 0.9 copy-done.2
  38.3 2.7 convolution_bitcast_fusion
  41.3 63.1 %all-reduce.3.cloned.1.call-done = f32[768,768]{1,0:T(8,128)} async-done(((f32[768,768]{1,0:T(8,128)}), f32[768,768]{1,0:T(8,128)}) %all-reduce.3.cloned.1.call-update) | async-done | bytes 2359312 | tf_op jit(solution)/shard_map/psum | solution.py:62
  104.3 2.4 select_reduce_fusion
  107.4 6.4 %multiply_add_fusion.1 = f32[768,768]{1,0:T(8,128)S(1)} fusion(f32[768,768]{1,0:T(8,128)} %all-reduce.3.cloned.1.call-done, f32[]{:T(128)S(6)} %mul.80), kind=kOutput, calls=%fused_computation.7 | convolution fusion | flops 2720858112 | bytes 4718596 | tf_op jit(solution)/shard_map/dot_general | solution.py:23
  113.9 3.2 %fusion.5 = f32[768,768]{1,0:T(8,128)S(1)} fusion(f32[768,768]{1,0:T(8,128)S(1)} %multiply_add_fusion.1, f32[768,768]{1,0:T(8,128)S(1)} %copy-done.4, f32[]{:T(128)S(6)} %mul.80), kind=kOutput, calls=%fused_computation.11 | convolution fusion | flops 2720268288 | bytes 7077892 | tf_op jit(solution)/shard_map/dot_general | solution.py:23
  117.0 3.2 %fusion.4 = f32[768,768]{1,0:T(8,128)S(1)} fusion(f32[768,768]{1,0:T(8,128)S(1)} %fusion.5, f32[768,768]{1,0:T(8,128)S(1)} %multiply_add_fusion.1), kind=kOutput, calls=%fused_computation.10 | convolution fusion | flops 2719678464 | bytes 7077888 | tf_op jit(solution)/shard_map/dot_general | solution.py:23
  120.2 3.5 %multiply_add_fusion = f32[768,768]{1,0:T(8,128)S(1)} fusion(f32[768,768]{1,0:T(8,128)S(1)} %fusion.4), kind=kOutput, calls=%fused_computation.6 | convolution fusion | flops 2719678464 | bytes 4718592 | tf_op jit(solution)/shard_map/dot_general | solution.py:23
  123.7 3.1 %fusion.7 = f32[768,768]{1,0:T(8,128)S(1)} fusion(f32[768,768]{1,0:T(8,128)S(1)} %fusion.4, f32[768,768]{1,0:T(8,128)S(1)} %multiply_add_fusion), kind=kOutput, calls=%fused_computation.13 | convolution fusion | flops 2719678464 | bytes 7077888 | tf_op jit(solution)/shard_map/dot_general | solution.py:23
  126.9 3.2 %fusion.6 = f32[768,768]{1,0:T(8,128)S(1)} fusion(f32[768,768]{1,0:T(8,128)S(1)} %fusion.7, f32[768,768]{1,0:T(8,128)S(1)} %multiply_add_fusion), kind=kOutput, calls=%fused_computation.12 | convolution fusion | flops 2719678464 | bytes 7077888 | tf_op jit(solution)/shard_map/dot_general | solution.py:23
  130.1 3.1 %fusion.36 = f32[768,768]{1,0:T(8,128)S(1)} fusion(f32[768,768]{1,0:T(8,128)S(1)} %fusion.6), kind=kOutput, calls=%fused_computation.55 | convolution fusion | flops 2717908992 | bytes 4718592 | tf_op jit(solution)/shard_map/dot_general | solution.py:23
  133.3 1.4 convolution_add_fusion.1
  134.7 1.4 convolution_add_fusion
  136.1 1.4 fusion.11
  137.5 0.9 copy-done.1
  139.1 3.8 %collective-permute-start = (f32[48,768]{1,0:T(8,128)}, f32[48,768]{1,0:T(8,128)}, u32[]{:S(2)}, u32[]{:S(2)}) collective-permute-start(f32[48,768]{1,0:T(8,128)} %slice.24), channel_id=1, source_target_pairs={{0,1},{2,3},{4,5},{6,7},{8,9},{10,11},{12,13},{14,15},{16,17},{18,... | collective-permute-start | bytes 442376 | tf_op jit(solution)/shard_map/ppermute | solution.py:90
  142.9 1.7 collective-permute-done
  145.4 1.0 slice.29
  146.4 1.3 collective-permute-start.1
  147.7 8.6 %collective-permute-done.1 = f32[128,768]{1,0:T(8,128)S(1)} collective-permute-done((f32[128,768]{1,0:T(8,128)S(1)}, f32[128,768]{1,0:T(8,128)S(1)}, u32[]{:S(2)}, u32[]{:S(2)}) %collective-permute-start.1) | collective-permute-done | bytes 393248 | tf_op jit(solution)/shard_map/ppermute | solution.py:91
  156.3 1.8 slice_select_fusion
  158.1 35.6 %all-gather.3.cloned.1.call-done = f32[768,768]{1,0:T(8,128)} async-done(((f32[48,768]{1,0:T(8,128)}), f32[768,768]{1,0:T(8,128)}) %all-gather.3.cloned.1.call-update) | async-done | bytes 2359312 | tf_op jit(solution)/shard_map/all_gather | solution.py:94
  193.7 64.6 %all-gather.5.cloned.1.call-done = f32[2048,768]{1,0:T(8,128)} async-done(((f32[128,768]{1,0:T(8,128)}), f32[2048,768]{1,0:T(8,128)}) %all-gather.5.cloned.1.call-update) | async-done | bytes 6291472 | tf_op jit(solution)/shard_map/all_gather | solution.py:95
  258.3 3.2 %copy.27 = f32[8,96,768]{2,1,0:T(8,128)} copy(f32[8,96,768]{2,1,0:T(8,128)} %bitcast.33) | data formatting | bytes 4718592
  261.5 5.9 %copy.28 = f32[8,256,768]{2,1,0:T(8,128)} copy(f32[8,256,768]{2,1,0:T(8,128)} %bitcast.29) | data formatting | bytes 12582912
  (22 shorter events, 2.9 us)
Async XLA Ops:
  7.2 6.2 %copy-start = (bf16[8,256,768]{2,1,0:T(8,128)(2,1)S(1)}, bf16[8,256,768]{2,1,0:T(8,128)(2,1)}, u32[]{:S(2)}) copy-start(bf16[8,256,768]{2,1,0:T(8,128)(2,1)} %param.5) | copy-start | bytes 9437188
  7.2 97.2 %all-reduce.3.cloned.1.call-start = ((), (), s32[]{:S(2)}) async-start(), calls=%async_computation.1 | async-start | bytes 4718592 | tf_op jit(solution)/shard_map/psum | solution.py:62
  37.5 0.9 copy-start.2
  41.0 152.7 %all-gather.3.cloned.1.call-start = ((), (), s32[]{:S(2)}) async-start(), calls=%async_computation.2 | async-start | bytes 2506752 | tf_op jit(solution)/shard_map/all_gather | solution.py:94
  107.4 6.5 %copy-start.4 = (f32[768,768]{1,0:T(8,128)S(1)}, f32[768,768]{1,0:T(8,128)}, u32[]{:S(2)}) copy-start(f32[768,768]{1,0:T(8,128)} %all-reduce.3.cloned.1.call-done) | copy-start | bytes 7077892
  130.0 3.2 %copy-start.3 = (f32[16,16,768]{2,1,0:T(8,128)S(1)}, f32[16,16,768]{2,1,0:T(8,128)}, u32[]{:S(2)}) copy-start(f32[16,16,768]{2,1,0:T(8,128)} %copy-done.2) | copy-start | bytes 2359300
  137.5 0.9 copy-start.1
  139.1 5.5 %collective-permute-start = (f32[48,768]{1,0:T(8,128)}, f32[48,768]{1,0:T(8,128)}, u32[]{:S(2)}, u32[]{:S(2)}) collective-permute-start(f32[48,768]{1,0:T(8,128)} %slice.24), channel_id=1, source_target_pairs={{0,1},{2,3},{4,5},{6,7},{8,9},{10,11},{12,13},{14,15},{16,17},{18,... | collective-permute-start | bytes 442376 | tf_op jit(solution)/shard_map/ppermute | solution.py:90
  145.3 113.0 %all-gather.5.cloned.1.call-start = ((), (), s32[]{:S(2)}) async-start(), calls=%async_computation.3 | async-start | bytes 6684672 | tf_op jit(solution)/shard_map/all_gather | solution.py:95
  146.4 9.9 %collective-permute-start.1 = (f32[128,768]{1,0:T(8,128)S(1)}, f32[128,768]{1,0:T(8,128)S(1)}, u32[]{:S(2)}, u32[]{:S(2)}) collective-permute-start(f32[128,768]{1,0:T(8,128)S(1)} %slice.29), channel_id=1, source_target_pairs={{1,0},{3,2},{5,4},{7,6},{9,8},{11,10},{13,12},{15,14},{17,16},{19,... | collective-permute-start | bytes 1179656 | tf_op jit(solution)/shard_map/ppermute | solution.py:91
Sparse Core Ops, SparseCore 0:
  41.2 63.1 all-reduce.2
  145.5 48.2 all-gather.2
  196.4 61.8 all-gather.4

commit v4 on v2

--- a/solution.py
+++ b/solution.py
@@ -59,10 +59,37 @@
     held = lax.all_to_all(send, "tensor", split_axis=0, concat_axis=0, tiled=True)
     rows = held.reshape(tensor_count * piece, held.shape[2])
 
-    gram = lax.psum(gram_of(rows), "shard")
-    columns = gram.shape[0]
+    part = gram_of(rows)
+    columns = part.shape[0]
+    half = columns // 2
+    assert 2 * half == columns and half % 8 == 0
+    row_id = lax.broadcasted_iota(jnp.int32, (half, half), 0)
+    col_id = lax.broadcasted_iota(jnp.int32, (half, half), 1)
+    upper = col_id >= row_id
+    on_diagonal = col_id == row_id
+    corner = part[half:, half:]
+    folded = jnp.where(upper, part[:half, :half], corner)
+    corner_diagonal = jnp.sum(jnp.where(on_diagonal, corner, 0.0), axis=0)
+    tail = jnp.zeros((8, half), jnp.float32).at[0].set(corner_diagonal)
+    packed = jnp.concatenate([part[:half, half:], folded, tail], axis=0)
+    packed = lax.psum(packed, "shard")
+    side = packed[:half]
+    folded = packed[half:columns]
+    corner_diagonal = packed[columns]
+    flipped = folded.T
+    top_left = jnp.where(upper, folded, flipped)
+    bottom_right = jnp.where(
+        on_diagonal, corner_diagonal[None, :], jnp.where(upper, flipped, folded)
+    )
+    gram = jnp.concatenate(
+        [
+            jnp.concatenate([top_left, side], axis=1),
+            jnp.concatenate([side.T, bottom_right], axis=1),
+        ],
+        axis=0,
+    )
+    total = jnp.sum(jnp.where(on_diagonal, folded, 0.0)) + jnp.sum(corner_diagonal)
     eye = jnp.eye(columns, dtype=jnp.float32)
-    total = jnp.sum(gram * eye)
     denom = jnp.sqrt(total) + epsilon
     current = rows / denom
     gram = gram / (denom * denom)

time: 249 us -> 253 us (1.016)
  local copies, waits for them, and re-layouts: 14.5 us -> 19.8 us
  waiting for transfers between devices: 155 us -> 150 us
  other arithmetic: 8.74 us -> 12.4 us
    psum x1, waiting for transfers between devices: 63.1 us -> 59 us  [shards(): packed = lax.psum(packed, 'shard')]
    slice x0 -> x2, local copies, waits for them, and re-layouts: none -> 4.03 us  [shards(): folded = packed[half:columns]]
    select_n x0 -> x1, other arithmetic: none -> 3.5 us  [shards(): top_left = jnp.where(upper, folded, flipped)]
where the time goes in v4:
time: 253 us
  waiting for transfers between devices  150 us (59%)
  matrix products  32.3 us (13%)
  blocking collectives  21.9 us (9%)
  local copies, waits for them, and re-layouts  19.8 us (8%)
  between operations  15.5 us (6%)
  other arithmetic  12.4 us (5%)
    all_gather x1, waiting for transfers between devices, shards(): gathered = lax.all_gather(update[None], 'tensor', axis=0, tiled=True)  91.4 us
    psum x1, waiting for transfers between devices, shards(): packed = lax.psum(packed, 'shard')  59 us
    dot_general x10, matrix products, dot(): jnp.dot(x, y, precision=PRECISION, preferred_element_type=jnp.float32)  31 us
    all_to_all x1, blocking collectives, shards(): lax.all_to_all(send, 'tensor', split_axis=0, concat_axis=0, tiled=True)  21.9 us
    slice x1, local copies, waits for them, and re-layouts, shards(): gathered[:, 1].reshape(count_wide, tensor_count * piece, update.shape[1])  5.94 us
  transfers between devices with their start and end apart: 2, of which 2 were waited for; matrix products, arithmetic and copies ran while one was open for 0% of the time, Pallas kernels for 0%

profile of v4, /device:TPU:1, one launch (start us, length us, event | category | flops | bytes accessed | tf_op | source)
XLA Modules:
  0.0 252.5 jit_solution(15665380829009407035)
XLA Ops:
  7.2 1.2 broadcast_multiply_fusion
  8.4 1.6 broadcast_multiply_fusion.1
  10.0 1.0 constant_dynamic-slice_fusion.1
  11.0 1.6 convert_add_fusion.3
  12.6 0.8 pad_bitcast_fusion
  13.4 0.9 convert_add_fusion.1
  14.2 1.0 pad_maximum_fusion
  15.3 0.3 copy.15
  15.5 21.9 %all_to_all.5 = f32[16,16,768]{2,1,0:T(8,128)S(1)} all-to-all(f32[16,16,768]{2,1,0:T(8,128)S(1)} %bitcast.40), channel_id=1, replica_groups=mesh['shard'=8,'tensor'=16] {'tensor'}, dimensions={0} | all-to-all | bytes 1572864 | tf_op jit(solution)/shard_map/all_to_all | solution.py:59
  37.5 1.3 convolution_bitcast_fusion
  38.9 1.1 select_maximum_fusion
  40.2 59.0 %all-reduce.4.cloned.1.call-done = f32[776,384]{1,0:T(8,128)} async-done(((f32[776,384]{1,0:T(8,128)}), f32[776,384]{1,0:T(8,128)}) %all-reduce.4.cloned.1.call-update) | async-done | bytes 1191952 | tf_op jit(solution)/shard_map/psum | solution.py:75
  99.2 1.9 slice.49
  101.1 2.1 copy.16
  103.2 1.3 slice_reduce_fusion
  104.5 3.5 %bitcast_select_fusion.1 = (f32[384,384]{1,0:T(8,128)}, f32[384,384]{1,0:T(8,128)}, f32[384,384]{0,1:T(8,128)}, f32[384,384]{1,0:T(8,128)}, f32[]{:T(128)}) fusion(f32[384,384]{0,1:T(8,128)} %copy.16, f32[776,384]{1,0:T(8,128)} %all-reduce.4.cloned.1.call-done, f32[384]{0:T(512)S(1)} %get-tuple-element.20), kind=kLoop, calls=%fused_computation.34 | loop fusion | flops 1032191 | bytes 4130308 | tf_op jit(solution)/shard_map/jit(_where)/select_n | solution.py:80
  108.0 2.1 copy.17
  111.4 6.4 %multiply_add_fusion.1 = f32[768,768]{1,0:T(8,128)S(1)} fusion(f32[]{:T(128)S(6)} %mul.76, f32[384,384]{1,0:T(8,128)} %get-tuple-element.26, f32[384,384]{1,0:T(8,128)} %copy.17, f32[384,384]{1,0:T(8,128)} %get-tuple-element.28, f32[384,384]{1,0:T(8,128)} %get-tuple-element.25), kind=kOutput, calls=%fused_computation.9 | convolution fusion | flops 2724397056 | bytes 4718596 | tf_op jit(solution)/shard_map/dot_general | solution.py:23
  117.9 3.2 %fusion.5 = f32[768,768]{1,0:T(8,128)S(1)} fusion(f32[768,768]{1,0:T(8,128)S(1)} %multiply_add_fusion.1, f32[384,384]{1,0:T(8,128)S(1)} %copy-done.5, f32[384,384]{1,0:T(8,128)S(1)} %copy-done.3, f32[384,384]{1,0:T(8,128)S(1)} %copy-done.6, f32[384,384]{1,0:T(8,128)S(1)} %copy-done.4, f32[]{:T(128)S(6)} %mul.76), kind=kOutput, calls=%fused_computation.11 | convolution fusion | flops 2722037760 | bytes 7077892 | tf_op jit(solution)/shard_map/dot_general | solution.py:23
  121.0 3.2 %fusion.4 = f32[768,768]{1,0:T(8,128)S(1)} fusion(f32[768,768]{1,0:T(8,128)S(1)} %fusion.5, f32[768,768]{1,0:T(8,128)S(1)} %multiply_add_fusion.1), kind=kOutput, calls=%fused_computation.10 | convolution fusion | flops 2719678464 | bytes 7077888 | tf_op jit(solution)/shard_map/dot_general | solution.py:23
  124.2 3.5 %multiply_add_fusion = f32[768,768]{1,0:T(8,128)S(1)} fusion(f32[768,768]{1,0:T(8,128)S(1)} %fusion.4), kind=kOutput, calls=%fused_computation.7 | convolution fusion | flops 2719678464 | bytes 4718592 | tf_op jit(solution)/shard_map/dot_general | solution.py:23
  127.7 3.1 %fusion.7 = f32[768,768]{1,0:T(8,128)S(1)} fusion(f32[768,768]{1,0:T(8,128)S(1)} %fusion.4, f32[768,768]{1,0:T(8,128)S(1)} %multiply_add_fusion), kind=kOutput, calls=%fused_computation.13 | convolution fusion | flops 2719678464 | bytes 7077888 | tf_op jit(solution)/shard_map/dot_general | solution.py:23
  130.9 3.2 %fusion.6 = f32[768,768]{1,0:T(8,128)S(1)} fusion(f32[768,768]{1,0:T(8,128)S(1)} %fusion.7, f32[768,768]{1,0:T(8,128)S(1)} %multiply_add_fusion), kind=kOutput, calls=%fused_computation.12 | convolution fusion | flops 2719678464 | bytes 7077888 | tf_op jit(solution)/shard_map/dot_general | solution.py:23
  134.1 3.1 %fusion.37 = f32[768,768]{1,0:T(8,128)S(1)} fusion(f32[768,768]{1,0:T(8,128)S(1)} %fusion.6), kind=kOutput, calls=%fused_computation.65 | convolution fusion | flops 2717908992 | bytes 4718592 | tf_op jit(solution)/shard_map/dot_general | solution.py:23
  137.3 1.4 convolution_add_fusion.1
  138.7 1.7 convolution_add_fusion
  140.4 2.3 fusion.11
  142.7 91.4 %all-gather.3.cloned.1.call-done = f32[4096,768]{1,0:T(8,128)} async-done(((f32[256,768]{1,0:T(8,128)}), f32[4096,768]{1,0:T(8,128)}) %all-gather.3.cloned.1.call-update) | async-done | bytes 12582928 | tf_op jit(solution)/shard_map/all_gather | solution.py:109
  234.1 2.2 slice.52
  236.3 5.9 %slice.53 = f32[8,1,16,16,768]{4,3,2,1,0:T(8,128)} slice(f32[8,2,16,16,768]{4,3,2,1,0:T(8,128)} %bitcast.38), slice={[0:8], [1:2], [0:16], [0:16], [0:768]} | slice | bytes 12582912 | tf_op jit(solution)/shard_map/slice | solution.py:114
  242.2 1.4 copy.22
  243.6 2.1 copy.19
  (22 shorter events, 0.5 us)
Async XLA Ops:
  7.2 6.2 %copy-start = (bf16[8,256,768]{2,1,0:T(8,128)(2,1)S(1)}, bf16[8,256,768]{2,1,0:T(8,128)(2,1)}, u32[]{:S(2)}) copy-start(bf16[8,256,768]{2,1,0:T(8,128)(2,1)} %param.7) | copy-start | bytes 9437188
  7.2 92.0 %all-reduce.4.cloned.1.call-start = ((), (), s32[]{:S(2)}) async-start(), calls=%async_computation.1 | async-start | bytes 2383872 | tf_op jit(solution)/shard_map/psum | solution.py:75
  37.5 1.3 copy-start.1
  40.0 194.1 %all-gather.3.cloned.1.call-start = ((), (), s32[]{:S(2)}) async-start(), calls=%async_computation.2 | async-start | bytes 13369344 | tf_op jit(solution)/shard_map/all_gather | solution.py:109
  111.4 6.4 %copy-start.3 = (f32[384,384]{1,0:T(8,128)S(1)}, f32[384,384]{1,0:T(8,128)}, u32[]{:S(2)}) copy-start(f32[384,384]{1,0:T(8,128)} %copy.17) | copy-start | bytes 1769476
  111.4 6.4 %copy-start.4 = (f32[384,384]{1,0:T(8,128)S(1)}, f32[384,384]{1,0:T(8,128)}, u32[]{:S(2)}) copy-start(f32[384,384]{1,0:T(8,128)} %get-tuple-element.25) | copy-start | bytes 1769476
  111.4 6.4 %copy-start.5 = (f32[384,384]{1,0:T(8,128)S(1)}, f32[384,384]{1,0:T(8,128)}, u32[]{:S(2)}) copy-start(f32[384,384]{1,0:T(8,128)} %get-tuple-element.26) | copy-start | bytes 1769476
  111.4 6.4 %copy-start.6 = (f32[384,384]{1,0:T(8,128)S(1)}, f32[384,384]{1,0:T(8,128)}, u32[]{:S(2)}) copy-start(f32[384,384]{1,0:T(8,128)} %get-tuple-element.28) | copy-start | bytes 1769476
  134.0 3.2 %copy-start.2 = (f32[16,16,768]{2,1,0:T(8,128)S(1)}, f32[16,16,768]{2,1,0:T(8,128)}, u32[]{:S(2)}) copy-start(f32[16,16,768]{2,1,0:T(8,128)} %copy-done.1) | copy-start | bytes 2359300
Sparse Core Ops, SparseCore 0:
  40.1 59.0 all-reduce.3
  142.8 91.2 all-gather.2

commit v5 on v2

--- a/solution.py
+++ b/solution.py
@@ -65,27 +65,41 @@
     total = jnp.sum(gram * eye)
     denom = jnp.sqrt(total) + epsilon
     current = rows / denom
-    gram = gram / (denom * denom)
+    shrink = 1.0 / (denom * denom)
     for iteration in range(ITERS):
         square_gram = dot(gram, gram)
-        mixer = coef_b * gram + coef_c * square_gram
+        if iteration == 0:
+            mixer = (coef_b * shrink) * gram + (coef_c * shrink * shrink) * square_gram
+        else:
+            mixer = coef_b * gram + coef_c * square_gram
         current = coef_a * current + dot(current, mixer)
         if iteration + 1 < ITERS:
             full = mixer + coef_a * eye
             gram = dot(full, dot(gram, full))
+            if iteration == 0:
+                gram = shrink * gram
 
     is_square = member % 2 == 0
     scale = jnp.where(
         is_square, jnp.float32(math.sqrt(D)), jnp.float32(math.sqrt(FF))
     )
     update = scale * current
-    gathered = lax.all_gather(update[None], "tensor", axis=0, tiled=True)
-    gathered = gathered.reshape(count_square, 2, tensor_count, piece, update.shape[1])
-    update_square = gathered[:, 0, :, : piece - pad].reshape(
-        count_square, tensor_count * (piece - pad), update.shape[1]
+    square_piece = piece - pad
+    square_rows = update.reshape(tensor_count, piece, -1)[:, :square_piece]
+    square_rows = square_rows.reshape(tensor_count * square_piece, -1)
+    wide_rows = update.shape[0]
+    chunk = (square_rows.shape[0] + wide_rows) // 2
+    assert 2 * chunk == square_rows.shape[0] + wide_rows
+    to_even = [(2 * j + 1, 2 * j) for j in range(count_square)]
+    handed = lax.ppermute(update[chunk:], "tensor", to_even)
+    mine = jnp.where(
+        is_square, jnp.concatenate([square_rows, handed], axis=0), update[:chunk]
     )
-    update_wide = gathered[:, 1].reshape(
-        count_wide, tensor_count * piece, update.shape[1]
+    gathered = lax.all_gather(mine, "tensor", axis=0, tiled=True)
+    gathered = gathered.reshape(count_square, 2, chunk, update.shape[1])
+    update_square = gathered[:, 0, : square_rows.shape[0]]
+    update_wide = jnp.concatenate(
+        [gathered[:, 1], gathered[:, 0, square_rows.shape[0]:]], axis=1
     )
     return (
         update_square,

time: 249 us -> 240 us (0.964)
  waiting for transfers between devices: 155 us -> 144 us
  other arithmetic: 8.74 us -> 12.4 us
  local copies, waits for them, and re-layouts: 14.5 us -> 11.9 us
    all_gather x1, waiting for transfers between devices: 91.5 us -> 75.9 us  [shards(): gathered = lax.all_gather(mine, 'tensor', axis=0, tiled=True)]
    squeeze x0 -> x3, local copies, waits for them, and re-layouts: none -> 7.45 us  [the longest x1 3.23 us: shards(): update_square = gathered[:, 0, :square_rows.shape[0]]]
    slice x2, local copies, waits for them, and re-layouts: 8.12 us -> 0.8 us  [the longest x1 0.77 us: shards(): handed = lax.ppermute(update[chunk:], 'tensor', to_even)]
    ppermute x0 -> x1, waiting for transfers between devices: none -> 5.15 us  [shards(): handed = lax.ppermute(update[chunk:], 'tensor', to_even)]
    unnamed x10, local copies, waits for them, and re-layouts: 4.39 us -> 0.91 us
    concatenate x0 -> x1, other arithmetic: none -> 3.17 us  [shards(): jnp.concatenate([gathered[:, 1], gathered[:, 0, square_rows.shape[0]:]],...]
  transfers between devices with their start and end apart: 2 -> 3, of which waited for: 2 -> 3; matrix products, arithmetic and copies ran while one was open for 0% -> 0% of each run, Pallas kernels for 0% -> 0%
where the time goes in v5:
time: 240 us; the launch traced here: 239 us
  waiting for transfers between devices  144 us (60%)
  matrix products  32.4 us (14%)
  blocking collectives  21.9 us (9%)
  between operations  15 us (6%)
  other arithmetic  12.4 us (5%)
  local copies, waits for them, and re-layouts  11.9 us (5%)
    all_gather x1, waiting for transfers between devices, shards(): gathered = lax.all_gather(mine, 'tensor', axis=0, tiled=True)  75.9 us
    psum x1, waiting for transfers between devices, shards(): gram = lax.psum(gram_of(rows), 'shard')  63.1 us
    dot_general x10, matrix products, dot(): jnp.dot(x, y, precision=PRECISION, preferred_element_type=jnp.float32)  29.8 us
    all_to_all x1, blocking collectives, shards(): lax.all_to_all(send, 'tensor', split_axis=0, concat_axis=0, tiled=True)  21.9 us
    ppermute x1, waiting for transfers between devices, shards(): handed = lax.ppermute(update[chunk:], 'tensor', to_even)  5.15 us
  transfers between devices with their start and end apart: 3, of which 3 were waited for; matrix products, arithmetic and copies ran while one was open for 0% of the time, Pallas kernels for 0%

profile of v5, /device:TPU:1, one launch (start us, length us, event | category | flops | bytes accessed | tf_op | source)
XLA Modules:
  0.0 239.4 jit_solution(10389374261952220848)
XLA Ops:
  7.2 1.1 broadcast_multiply_fusion.1
  8.3 1.0 constant_dynamic-slice_fusion.1
  9.3 0.7 convert_add_fusion.3
  10.0 0.8 pad_bitcast_fusion
  10.7 1.0 broadcast_multiply_fusion
  11.8 0.9 convert_add_fusion.1
  12.7 1.0 pad_maximum_fusion.1
  14.0 21.9 %all_to_all.5 = f32[16,16,768]{2,1,0:T(8,128)S(1)} all-to-all(f32[16,16,768]{2,1,0:T(8,128)S(1)} %bitcast.44), channel_id=1, replica_groups=mesh['shard'=8,'tensor'=16] {'tensor'}, dimensions={0} | all-to-all | bytes 1572864 | tf_op jit(solution)/shard_map/all_to_all | solution.py:59
  35.9 0.9 copy-done.3
  36.8 2.7 %convolution_bitcast_fusion = f32[768,768]{1,0:T(8,128)} fusion(f32[16,16,768]{2,1,0:T(8,128)S(1)} %all_to_all.5), kind=kOutput, calls=%fused_computation.21 | convolution fusion | flops 905969664 | bytes 3145728 | tf_op jit(solution)/shard_map/dot_general | solution.py:27
  39.7 63.1 %all-reduce.3.cloned.1.call-done = f32[768,768]{1,0:T(8,128)} async-done(((f32[768,768]{1,0:T(8,128)}), f32[768,768]{1,0:T(8,128)}) %all-reduce.3.cloned.1.call-update) | async-done | bytes 2359312 | tf_op jit(solution)/shard_map/psum | solution.py:62
  102.8 2.4 select_reduce_fusion
  106.0 6.3 %multiply_add_fusion.1 = f32[768,768]{1,0:T(8,128)S(1)} fusion(f32[768,768]{1,0:T(8,128)} %all-reduce.3.cloned.1.call-done, f32[]{:T(128)S(6)} %mul.106, f32[]{:T(128)S(6)} %mul.102), kind=kOutput, calls=%fused_computation.10 | convolution fusion | flops 2719678464 | bytes 4718600 | tf_op jit(solution)/shard_map/dot_general | solution.py:23
  112.3 3.1 %fusion.11 = f32[768,768]{1,0:T(8,128)S(1)} fusion(f32[768,768]{1,0:T(8,128)S(1)} %copy-done.1, f32[768,768]{1,0:T(8,128)S(1)} %multiply_add_fusion.1), kind=kOutput, calls=%fused_computation.19 | convolution fusion | flops 2719678464 | bytes 7077888 | tf_op jit(solution)/shard_map/dot_general | solution.py:23
  115.5 3.2 %fusion.10 = f32[768,768]{1,0:T(8,128)S(1)} fusion(f32[768,768]{1,0:T(8,128)S(1)} %fusion.11, f32[768,768]{1,0:T(8,128)S(1)} %multiply_add_fusion.1), kind=kOutput, calls=%fused_computation.18 | convolution fusion | flops 2719678464 | bytes 7077888 | tf_op jit(solution)/shard_map/dot_general | solution.py:23
  118.8 1.4 convolution_add_fusion.1
  120.2 3.5 %multiply_add_fusion = f32[768,768]{1,0:T(8,128)S(1)} fusion(f32[768,768]{1,0:T(8,128)S(1)} %fusion.10, f32[]{:T(128)S(6)} %div.15), kind=kOutput, calls=%fused_computation.9 | convolution fusion | flops 2720858112 | bytes 4718596 | tf_op jit(solution)/shard_map/dot_general | solution.py:23
  123.6 3.2 %fusion.4 = f32[768,768]{1,0:T(8,128)S(1)} fusion(f32[768,768]{1,0:T(8,128)S(1)} %fusion.10, f32[768,768]{1,0:T(8,128)S(1)} %multiply_add_fusion, f32[]{:T(128)S(6)} %div.15), kind=kOutput, calls=%fused_computation.13 | convolution fusion | flops 2720268288 | bytes 7077892 | tf_op jit(solution)/shard_map/dot_general | solution.py:23
  126.8 3.2 %fusion.12 = f32[768,768]{1,0:T(8,128)S(1)} fusion(f32[768,768]{1,0:T(8,128)S(1)} %fusion.4, f32[768,768]{1,0:T(8,128)S(1)} %multiply_add_fusion), kind=kOutput, calls=%fused_computation.20 | convolution fusion | flops 2719678464 | bytes 7077888 | tf_op jit(solution)/shard_map/dot_general | solution.py:23
  130.0 1.4 convolution_add_fusion
  131.4 3.1 %fusion.42 = f32[768,768]{1,0:T(8,128)S(1)} fusion(f32[768,768]{1,0:T(8,128)S(1)} %fusion.12), kind=kOutput, calls=%fused_computation.61 | convolution fusion | flops 2717908992 | bytes 4718592 | tf_op jit(solution)/shard_map/dot_general | solution.py:23
  134.5 1.4 fusion.16
  135.9 0.8 slice.25
  136.7 1.3 collective-permute-start
  138.0 0.8 reshape.37
  138.8 5.1 %collective-permute-done = f32[80,768]{1,0:T(8,128)} collective-permute-done((f32[80,768]{1,0:T(8,128)}, f32[80,768]{1,0:T(8,128)}, u32[]{:S(2)}, u32[]{:S(2)}) %collective-permute-start) | collective-permute-done | bytes 245792 | tf_op jit(solution)/shard_map/ppermute | solution.py:94
  144.0 2.1 slice_select_fusion
  146.0 75.9 %all-gather.2.cloned.1.call-done = f32[2816,768]{1,0:T(8,128)} async-done(((f32[176,768]{1,0:T(8,128)}), f32[2816,768]{1,0:T(8,128)}) %all-gather.2.cloned.1.call-update) | async-done | bytes 8650768 | tf_op jit(solution)/shard_map/all_gather | solution.py:98
  221.9 1.7 slice_bitcast_fusion.2
  223.6 3.2 %slice_bitcast_fusion.1 = f32[8,96,768]{2,1,0:T(8,128)} fusion(f32[8,2,176,768]{3,2,1,0:T(8,128)} %bitcast.41), kind=kLoop, calls=%fused_computation.4 | loop fusion | bytes 4718592 | tf_op jit(solution)/shard_map/squeeze | solution.py:100
  226.8 2.5 %slice_bitcast_fusion = f32[8,176,768]{2,1,0:T(8,128)S(1)} fusion(f32[8,2,176,768]{3,2,1,0:T(8,128)} %bitcast.42), kind=kLoop, calls=%fused_computation.1 | loop fusion | bytes 8650752 | tf_op jit(solution)/shard_map/squeeze | solution.py:102
  229.4 3.2 %pad_maximum_fusion = f32[8,256,768]{2,1,0:T(8,128)} fusion(f32[8,80,768]{2,1,0:T(8,128)S(1)} %slice_bitcast_fusion.2, f32[8,176,768]{2,1,0:T(8,128)S(1)} %slice_bitcast_fusion), kind=kLoop, calls=%fused_computation | loop fusion | flops 1572864 | bytes 12582912 | tf_op jit(solution)/shard_map/concatenate | solution.py:101
  (17 shorter events, 0.7 us)
Async XLA Ops:
  7.2 4.6 %copy-start = (bf16[8,256,768]{2,1,0:T(8,128)(2,1)S(1)}, bf16[8,256,768]{2,1,0:T(8,128)(2,1)}, u32[]{:S(2)}) copy-start(bf16[8,256,768]{2,1,0:T(8,128)(2,1)} %param.5) | copy-start | bytes 9437188
  7.2 95.7 %all-reduce.3.cloned.1.call-start = ((), (), s32[]{:S(2)}) async-start(), calls=%async_computation.1 | async-start | bytes 4718592 | tf_op jit(solution)/shard_map/psum | solution.py:62
  35.9 0.9 copy-start.3
  39.5 182.4 %all-gather.2.cloned.1.call-start = ((), (), s32[]{:S(2)}) async-start(), calls=%async_computation.2 | async-start | bytes 9191424 | tf_op jit(solution)/shard_map/all_gather | solution.py:98
  106.0 6.4 %copy-start.1 = (f32[768,768]{1,0:T(8,128)S(1)}, f32[768,768]{1,0:T(8,128)}, u32[]{:S(2)}) copy-start(f32[768,768]{1,0:T(8,128)} %all-reduce.3.cloned.1.call-done) | copy-start | bytes 7077892
  115.5 3.2 %copy-start.4 = (f32[16,16,768]{2,1,0:T(8,128)S(1)}, f32[16,16,768]{2,1,0:T(8,128)}, u32[]{:S(2)}) copy-start(f32[16,16,768]{2,1,0:T(8,128)} %copy-done.3) | copy-start | bytes 2359300
  135.9 2.1 copy-start.2
  136.7 7.2 %collective-permute-start = (f32[80,768]{1,0:T(8,128)}, f32[80,768]{1,0:T(8,128)}, u32[]{:S(2)}, u32[]{:S(2)}) collective-permute-start(f32[80,768]{1,0:T(8,128)} %slice.25), channel_id=1, source_target_pairs={{1,0},{3,2},{5,4},{7,6},{9,8},{11,10},{13,12},{15,14},{17,16},{19,... | collective-permute-start | bytes 737288 | tf_op jit(solution)/shard_map/ppermute | solution.py:94
Sparse Core Ops, SparseCore 0:
  39.6 63.1 all-reduce.2
  146.2 75.6 all-gather.1

commit v6 on v5

--- a/solution.py
+++ b/solution.py
@@ -53,7 +53,7 @@
     piece = look_wide.shape[1]
     pad = piece - look_square.shape[1]
     padded_square = jnp.pad(look_square, ((0, 0), (0, pad), (0, 0)))
-    send = jnp.stack([padded_square, look_wide], axis=1).reshape(
+    send = jnp.stack([look_wide, padded_square], axis=1).reshape(
         tensor_count, piece, look_wide.shape[2]
     )
     held = lax.all_to_all(send, "tensor", split_axis=0, concat_axis=0, tiled=True)
@@ -79,7 +79,7 @@
             if iteration == 0:
                 gram = shrink * gram
 
-    is_square = member % 2 == 0
+    is_square = member % 2 == 1
     scale = jnp.where(
         is_square, jnp.float32(math.sqrt(D)), jnp.float32(math.sqrt(FF))
     )
@@ -90,17 +90,15 @@
     wide_rows = update.shape[0]
     chunk = (square_rows.shape[0] + wide_rows) // 2
     assert 2 * chunk == square_rows.shape[0] + wide_rows
-    to_even = [(2 * j + 1, 2 * j) for j in range(count_square)]
-    handed = lax.ppermute(update[chunk:], "tensor", to_even)
+    to_odd = [(2 * j, 2 * j + 1) for j in range(count_square)]
+    handed = lax.ppermute(update[chunk:], "tensor", to_odd)
     mine = jnp.where(
-        is_square, jnp.concatenate([square_rows, handed], axis=0), update[:chunk]
+        is_square, jnp.concatenate([handed, square_rows], axis=0), update[:chunk]
     )
     gathered = lax.all_gather(mine, "tensor", axis=0, tiled=True)
-    gathered = gathered.reshape(count_square, 2, chunk, update.shape[1])
-    update_square = gathered[:, 0, : square_rows.shape[0]]
-    update_wide = jnp.concatenate(
-        [gathered[:, 1], gathered[:, 0, square_rows.shape[0]:]], axis=1
-    )
+    gathered = gathered.reshape(count_square, 2 * chunk, update.shape[1])
+    update_wide = gathered[:, :wide_rows]
+    update_square = gathered[:, wide_rows:]
     return (
         update_square,
         update_wide,

time: 240 us -> 238 us (level)
  other arithmetic: 12.4 us -> 9.22 us
  waiting for transfers between devices: 144 us -> 141 us
  starting transfers between devices: 1.54 us -> 4.06 us
    slice x1 -> x3, local copies, waits for them, and re-layouts: 0.77 us -> 9.93 us  [the longest x1 5.94 us: shards(): update_wide = gathered[:, :wide_rows]]
    squeeze x3 -> x0, local copies, waits for them, and re-layouts: 7.45 us -> none  [the longest x1 3.23 us: shards(): update_square = gathered[:, 0, :square_rows.shape[0]]]
    ppermute x1, waiting for transfers between devices: 5.15 us -> 1.95 us  [shards(): handed = lax.ppermute(update[chunk:], 'tensor', to_odd)]
    concatenate x1 -> x0, other arithmetic: 3.17 us -> none  [shards(): jnp.concatenate([gathered[:, 1], gathered[:, 0, square_rows.shape[0]:]],...]
    ppermute x1, starting transfers between devices: 1.28 us -> 3.8 us  [shards(): handed = lax.ppermute(update[chunk:], 'tensor', to_odd)]
where the time goes in v6:
time: 238 us
  waiting for transfers between devices  141 us (59%)
  matrix products  32.4 us (14%)
  blocking collectives  21.9 us (9%)
  between operations  15 us (6%)
  local copies, waits for them, and re-layouts  13.7 us (6%)
  other arithmetic  9.22 us (4%)
  starting transfers between devices  4.06 us (2%)
    all_gather x1, waiting for transfers between devices, shards(): gathered = lax.all_gather(mine, 'tensor', axis=0, tiled=True)  76.3 us
    psum x1, waiting for transfers between devices, shards(): gram = lax.psum(gram_of(rows), 'shard')  63.1 us
    dot_general x10, matrix products, dot(): jnp.dot(x, y, precision=PRECISION, preferred_element_type=jnp.float32)  29.8 us
    all_to_all x1, blocking collectives, shards(): lax.all_to_all(send, 'tensor', split_axis=0, concat_axis=0, tiled=True)  21.9 us
    slice x1, local copies, waits for them, and re-layouts, shards(): update_wide = gathered[:, :wide_rows]  5.94 us
  transfers between devices with their start and end apart: 3, of which 3 were waited for; matrix products, arithmetic and copies ran while one was open for 0% of the time, Pallas kernels for 0%

profile of v6, /device:TPU:1, one launch (start us, length us, event | category | flops | bytes accessed | tf_op | source)
XLA Modules:
  0.0 237.6 jit_solution(12381198506008649817)
XLA Ops:
  7.2 1.1 broadcast_multiply_fusion.1
  8.3 1.0 constant_dynamic-slice_fusion
  9.3 0.7 convert_add_fusion.3
  10.0 0.8 pad_bitcast_fusion
  10.7 1.0 broadcast_multiply_fusion
  11.8 0.9 convert_add_fusion.1
  12.7 1.0 pad_maximum_fusion
  13.7 0.3 copy.13
  14.0 21.9 %all_to_all.5 = f32[16,16,768]{2,1,0:T(8,128)S(1)} all-to-all(f32[16,16,768]{2,1,0:T(8,128)S(1)} %bitcast.31), channel_id=1, replica_groups=mesh['shard'=8,'tensor'=16] {'tensor'}, dimensions={0} | all-to-all | bytes 1572864 | tf_op jit(solution)/shard_map/all_to_all | solution.py:59
  35.9 0.9 copy-done.3
  36.8 2.7 %convolution_bitcast_fusion = f32[768,768]{1,0:T(8,128)} fusion(f32[16,16,768]{2,1,0:T(8,128)S(1)} %all_to_all.5), kind=kOutput, calls=%fused_computation.17 | convolution fusion | flops 905969664 | bytes 3145728 | tf_op jit(solution)/shard_map/dot_general | solution.py:27
  39.5 0.2 all-gather.2.cloned.1.call-start
  39.7 63.1 %all-reduce.3.cloned.1.call-done = f32[768,768]{1,0:T(8,128)} async-done(((f32[768,768]{1,0:T(8,128)}), f32[768,768]{1,0:T(8,128)}) %all-reduce.3.cloned.1.call-update) | async-done | bytes 2359312 | tf_op jit(solution)/shard_map/psum | solution.py:62
  102.8 2.4 select_reduce_fusion
  105.9 6.3 %multiply_add_fusion.1 = f32[768,768]{1,0:T(8,128)S(1)} fusion(f32[768,768]{1,0:T(8,128)} %all-reduce.3.cloned.1.call-done, f32[]{:T(128)S(6)} %mul.106, f32[]{:T(128)S(6)} %mul.102), kind=kOutput, calls=%fused_computation.7 | convolution fusion | flops 2719678464 | bytes 4718600 | tf_op jit(solution)/shard_map/dot_general | solution.py:23
  112.3 3.1 %fusion.11 = f32[768,768]{1,0:T(8,128)S(1)} fusion(f32[768,768]{1,0:T(8,128)S(1)} %copy-done.1, f32[768,768]{1,0:T(8,128)S(1)} %multiply_add_fusion.1), kind=kOutput, calls=%fused_computation.15 | convolution fusion | flops 2719678464 | bytes 7077888 | tf_op jit(solution)/shard_map/dot_general | solution.py:23
  115.4 3.2 %fusion.10 = f32[768,768]{1,0:T(8,128)S(1)} fusion(f32[768,768]{1,0:T(8,128)S(1)} %fusion.11, f32[768,768]{1,0:T(8,128)S(1)} %multiply_add_fusion.1), kind=kOutput, calls=%fused_computation.14 | convolution fusion | flops 2719678464 | bytes 7077888 | tf_op jit(solution)/shard_map/dot_general | solution.py:23
  118.7 1.4 convolution_add_fusion.1
  120.1 3.5 %multiply_add_fusion = f32[768,768]{1,0:T(8,128)S(1)} fusion(f32[768,768]{1,0:T(8,128)S(1)} %fusion.10, f32[]{:T(128)S(6)} %div.15), kind=kOutput, calls=%fused_computation.6 | convolution fusion | flops 2720858112 | bytes 4718596 | tf_op jit(solution)/shard_map/dot_general | solution.py:23
  123.6 3.2 %fusion.4 = f32[768,768]{1,0:T(8,128)S(1)} fusion(f32[768,768]{1,0:T(8,128)S(1)} %fusion.10, f32[768,768]{1,0:T(8,128)S(1)} %multiply_add_fusion, f32[]{:T(128)S(6)} %div.15), kind=kOutput, calls=%fused_computation.10 | convolution fusion | flops 2720268288 | bytes 7077892 | tf_op jit(solution)/shard_map/dot_general | solution.py:23
  126.8 3.2 %fusion.12 = f32[768,768]{1,0:T(8,128)S(1)} fusion(f32[768,768]{1,0:T(8,128)S(1)} %fusion.4, f32[768,768]{1,0:T(8,128)S(1)} %multiply_add_fusion), kind=kOutput, calls=%fused_computation.16 | convolution fusion | flops 2719678464 | bytes 7077888 | tf_op jit(solution)/shard_map/dot_general | solution.py:23
  129.9 1.4 convolution_add_fusion
  131.3 3.1 %fusion.42 = f32[768,768]{1,0:T(8,128)S(1)} fusion(f32[768,768]{1,0:T(8,128)S(1)} %fusion.12), kind=kOutput, calls=%fused_computation.57 | convolution fusion | flops 2717908992 | bytes 4718592 | tf_op jit(solution)/shard_map/dot_general | solution.py:23
  134.5 1.4 fusion.16
  135.9 0.8 slice.20
  136.7 3.8 %collective-permute-start = (f32[80,768]{1,0:T(8,128)}, f32[80,768]{1,0:T(8,128)}, u32[]{:S(2)}, u32[]{:S(2)}) collective-permute-start(f32[80,768]{1,0:T(8,128)} %slice.20), channel_id=1, source_target_pairs={{0,1},{2,3},{4,5},{6,7},{8,9},{10,11},{12,13},{14,15},{16,17},{18,... | collective-permute-start | bytes 737288 | tf_op jit(solution)/shard_map/ppermute | solution.py:94
  140.5 0.8 reshape.37
  141.3 1.9 collective-permute-done
  143.2 2.1 slice_select_fusion
  145.3 76.3 %all-gather.2.cloned.1.call-done = f32[2816,768]{1,0:T(8,128)} async-done(((f32[176,768]{1,0:T(8,128)}), f32[2816,768]{1,0:T(8,128)}) %all-gather.2.cloned.1.call-update) | async-done | bytes 8650768 | tf_op jit(solution)/shard_map/all_gather | solution.py:98
  221.6 3.2 %slice.23 = f32[8,96,768]{2,1,0:T(8,128)} slice(f32[8,352,768]{2,1,0:T(8,128)} %bitcast.28), slice={[0:8], [256:352], [0:768]} | slice | bytes 4718592 | tf_op jit(solution)/shard_map/slice | solution.py:101
  224.8 5.9 %slice.24 = f32[8,256,768]{2,1,0:T(8,128)} slice(f32[8,352,768]{2,1,0:T(8,128)} %bitcast.29), slice={[0:8], [0:256], [0:768]} | slice | bytes 12582912 | tf_op jit(solution)/shard_map/slice | solution.py:100
  (15 shorter events, 0.2 us)
Async XLA Ops:
  7.2 4.6 %copy-start = (bf16[8,256,768]{2,1,0:T(8,128)(2,1)S(1)}, bf16[8,256,768]{2,1,0:T(8,128)(2,1)}, u32[]{:S(2)}) copy-start(bf16[8,256,768]{2,1,0:T(8,128)(2,1)} %param.5) | copy-start | bytes 9437188
  7.2 95.6 %all-reduce.3.cloned.1.call-start = ((), (), s32[]{:S(2)}) async-start(), calls=%async_computation.1 | async-start | bytes 4718592 | tf_op jit(solution)/shard_map/psum | solution.py:62
  35.9 0.9 copy-start.3
  39.5 182.1 %all-gather.2.cloned.1.call-start = ((), (), s32[]{:S(2)}) async-start(), calls=%async_computation.2 | async-start | bytes 9191424 | tf_op jit(solution)/shard_map/all_gather | solution.py:98
  105.9 6.4 %copy-start.1 = (f32[768,768]{1,0:T(8,128)S(1)}, f32[768,768]{1,0:T(8,128)}, u32[]{:S(2)}) copy-start(f32[768,768]{1,0:T(8,128)} %all-reduce.3.cloned.1.call-done) | copy-start | bytes 7077892
  115.4 3.2 %copy-start.4 = (f32[16,16,768]{2,1,0:T(8,128)S(1)}, f32[16,16,768]{2,1,0:T(8,128)}, u32[]{:S(2)}) copy-start(f32[16,16,768]{2,1,0:T(8,128)} %copy-done.3) | copy-start | bytes 2359300
  135.9 4.6 %copy-start.2 = (f32[256,768]{1,0:T(8,128)}, f32[256,768]{1,0:T(8,128)S(1)}, u32[]{:S(2)}) copy-start(f32[256,768]{1,0:T(8,128)S(1)} %fusion.16) | copy-start | bytes 2359300
  136.7 6.5 %collective-permute-start = (f32[80,768]{1,0:T(8,128)}, f32[80,768]{1,0:T(8,128)}, u32[]{:S(2)}, u32[]{:S(2)}) collective-permute-start(f32[80,768]{1,0:T(8,128)} %slice.20), channel_id=1, source_target_pairs={{0,1},{2,3},{4,5},{6,7},{8,9},{10,11},{12,13},{14,15},{16,17},{18,... | collective-permute-start | bytes 737288 | tf_op jit(solution)/shard_map/ppermute | solution.py:94
Sparse Core Ops, SparseCore 0:
  39.6 63.1 all-reduce.2
  145.4 76.1 all-gather.1

commit v7 on v6

--- a/solution.py
+++ b/solution.py
@@ -33,6 +33,33 @@
     )
 
 
+def halving_psum(values, axis):
+    count = lax.axis_size(axis)
+    me = lax.axis_index(axis)
+    steps = count.bit_length() - 1
+    assert 1 << steps == count and values.shape[0] % count == 0
+    held = values
+    for level in range(steps):
+        step = 1 << level
+        half = held.shape[0] // 2
+        upper = (me // step) % 2
+        keep = lax.dynamic_slice_in_dim(held, upper * half, half, 0)
+        give = lax.dynamic_slice_in_dim(held, (1 - upper) * half, half, 0)
+        pairs = [(i, i ^ step) for i in range(count)]
+        held = keep + lax.ppermute(give, axis, pairs)
+    for level in reversed(range(steps)):
+        step = 1 << level
+        upper = (me // step) % 2
+        pairs = [(i, i ^ step) for i in range(count)]
+        got = lax.ppermute(held, axis, pairs)
+        held = jnp.where(
+            upper == 1,
+            jnp.concatenate([got, held], axis=0),
+            jnp.concatenate([held, got], axis=0),
+        )
+    return held
+
+
 def own_rows(grad, member, tensor_count):
     row_piece = grad.shape[1] // tensor_count
     return lax.dynamic_slice_in_dim(grad, member * row_piece, row_piece, 1)
@@ -59,7 +86,7 @@
     held = lax.all_to_all(send, "tensor", split_axis=0, concat_axis=0, tiled=True)
     rows = held.reshape(tensor_count * piece, held.shape[2])
 
-    gram = lax.psum(gram_of(rows), "shard")
+    gram = halving_psum(gram_of(rows), "shard")
     columns = gram.shape[0]
     eye = jnp.eye(columns, dtype=jnp.float32)
     total = jnp.sum(gram * eye)

time: 238 us -> 248 us (1.042)
  blocking collectives: 21.9 us -> 0 us
  starting transfers between devices: 4.06 us -> 25.5 us
  other arithmetic: 9.22 us -> 20 us
  waiting for transfers between devices: 141 us -> 131 us
  matrix products: 32.4 us -> 37.7 us
  local copies, waits for them, and re-layouts: 13.7 us -> 18.8 us
    psum x1 -> x0, waiting for transfers between devices: 63.1 us -> none  [shards(): gram = lax.psum(gram_of(rows), 'shard')]
    ppermute x0 -> x6, waiting for transfers between devices: none -> 41.8 us  [the longest x3 22.6 us: halving_psum(): held = keep + lax.ppermute(give, axis, pairs)]
    all_to_all x1 -> x0, blocking collectives: 21.9 us -> none  [shards(): lax.all_to_all(send, 'tensor', split_axis=0, concat_axis=0, tiled=True)]
    ppermute x0 -> x6, starting transfers between devices: none -> 14.1 us  [the longest x3 7.84 us: halving_psum(): got = lax.ppermute(held, axis, pairs)]
    all_to_all x0 -> x1, waiting for transfers between devices: none -> 13.2 us  [shards(): lax.all_to_all(send, 'tensor', split_axis=0, concat_axis=0, tiled=True)]
    all_to_all x0 -> x1, starting transfers between devices: none -> 8.63 us  [shards(): lax.all_to_all(send, 'tensor', split_axis=0, concat_axis=0, tiled=True)]
    dot_general x10, matrix products: 29.8 us -> 35 us  [dot(): jnp.dot(x, y, precision=PRECISION, preferred_element_type=jnp.float32)]
    select_n x0 -> x2, other arithmetic: none -> 4.78 us  [halving_psum(): jnp.where(upper == 1, jnp.concatenate([got, held], axis=0), jnp.concatena...]
  transfers between devices with their start and end apart: 3 -> 9, of which waited for: 3 -> 9; matrix products, arithmetic and copies ran while one was open for 0% -> 0% of each run, Pallas kernels for 0% -> 0%
where the time goes in v7:
time: 248 us
  waiting for transfers between devices  131 us (53%)
  matrix products  37.7 us (15%)
  starting transfers between devices  25.5 us (10%)
  other arithmetic  20 us (8%)
  local copies, waits for them, and re-layouts  18.8 us (8%)
  between operations  15 us (6%)
    all_gather x1, waiting for transfers between devices, shards(): gathered = lax.all_gather(mine, 'tensor', axis=0, tiled=True)  71.9 us
    dot_general x10, matrix products, dot(): jnp.dot(x, y, precision=PRECISION, preferred_element_type=jnp.float32)  35 us
    ppermute x3, waiting for transfers between devices, halving_psum(): held = keep + lax.ppermute(give, axis, pairs)  22.6 us
    ppermute x3, waiting for transfers between devices, halving_psum(): got = lax.ppermute(held, axis, pairs)  19.2 us
    all_to_all x1, waiting for transfers between devices, shards(): lax.all_to_all(send, 'tensor', split_axis=0, concat_axis=0, tiled=True)  13.2 us
    all_to_all x1, starting transfers between devices, shards(): lax.all_to_all(send, 'tensor', split_axis=0, concat_axis=0, tiled=True)  8.63 us
    ppermute x3, starting transfers between devices, halving_psum(): got = lax.ppermute(held, axis, pairs)  7.84 us
    ppermute x3, starting transfers between devices, halving_psum(): held = keep + lax.ppermute(give, axis, pairs)  6.28 us
  transfers between devices with their start and end apart: 9, of which 9 were waited for; matrix products, arithmetic and copies ran while one was open for 0% of the time, Pallas kernels for 0%

profile of v7, /device:TPU:1, one launch (start us, length us, event | category | flops | bytes accessed | tf_op | source)
XLA Modules:
  0.0 247.7 jit_solution(1209879026700578217)
XLA Ops:
  14.8 8.6 %all-to-all-start = ((f32[16,16,768]{2,1,0:T(8,128)}), f32[16,16,768]{2,1,0:T(8,128)}, u32[]{:S(2)}, u32[]{:S(2)}) async-start(f32[16,16,768]{2,1,0:T(8,128)} %bitcast.28), calls=%async_computation | async-start | bytes 1572864 | tf_op jit(solution)/shard_map/all_to_all | solution.py:86
  23.5 13.2 %all-to-all-done = f32[16,16,768]{2,1,0:T(8,128)} async-done(((f32[16,16,768]{2,1,0:T(8,128)}), f32[16,16,768]{2,1,0:T(8,128)}, u32[]{:S(2)}, u32[]{:S(2)}) %all-to-all-start) | async-done | bytes 786464 | tf_op jit(solution)/shard_map/all_to_all | solution.py:86
  36.8 2.7 %convolution_bitcast_fusion = f32[768,768]{1,0:T(8,128)S(1)} fusion(f32[16,16,768]{2,1,0:T(8,128)} %all-to-all-done), kind=kOutput, calls=%fused_computation.18 | convolution fusion | flops 905969664 | bytes 3145728 | tf_op jit(solution)/shard_map/dot_general | solution.py:27
  39.4 1.4 copy-done.3
  41.9 2.2 collective-permute-start
  44.1 2.8 %collective-permute-done = f32[384,768]{1,0:T(8,128)} collective-permute-done((f32[384,768]{1,0:T(8,128)}, f32[384,768]{1,0:T(8,128)}, u32[]{:S(2)}, u32[]{:S(2)}) %collective-permute-start) | collective-permute-done | bytes 1179680 | tf_op jit(solution)/shard_map/ppermute | solution.py:49
  47.0 1.8 dynamic-slice_add_fusion
  51.8 13.6 %collective-permute-done.1 = f32[192,768]{1,0:T(8,128)} collective-permute-done((f32[192,768]{1,0:T(8,128)}, f32[192,768]{1,0:T(8,128)}, u32[]{:S(2)}, u32[]{:S(2)}) %collective-permute-start.1) | collective-permute-done | bytes 589856 | tf_op jit(solution)/shard_map/ppermute | solution.py:49
  67.6 2.8 %collective-permute-start.2 = (f32[96,768]{1,0:T(8,128)S(1)}, f32[96,768]{1,0:T(8,128)}, u32[]{:S(2)}, u32[]{:S(2)}) collective-permute-start(f32[96,768]{1,0:T(8,128)S(1)} %constant_dynamic-slice_fusion), channel_id=1, source_target_pairs={{0,64},{16,80},{32,96},{48,112},{64,0},{80,16},{96,32},{112,48},{1... | collective-permute-start | bytes 884744 | tf_op jit(solution)/shard_map/ppermute | solution.py:49
  70.4 6.2 %collective-permute-done.2 = f32[96,768]{1,0:T(8,128)} collective-permute-done((f32[96,768]{1,0:T(8,128)S(1)}, f32[96,768]{1,0:T(8,128)}, u32[]{:S(2)}, u32[]{:S(2)}) %collective-permute-start.2) | collective-permute-done | bytes 294944 | tf_op jit(solution)/shard_map/ppermute | solution.py:49
  77.7 2.8 %collective-permute-start.3 = (f32[96,768]{1,0:T(8,128)S(1)}, f32[96,768]{1,0:T(8,128)}, u32[]{:S(2)}, u32[]{:S(2)}) collective-permute-start(f32[96,768]{1,0:T(8,128)S(1)} %dynamic-slice_add_fusion.2), channel_id=1, source_target_pairs={{0,64},{16,80},{32,96},{48,112},{64,0},{80,16},{96,32},{112,48},{1... | collective-permute-start | bytes 884744 | tf_op jit(solution)/shard_map/ppermute | solution.py:54
  80.5 5.3 %collective-permute-done.3 = f32[96,768]{1,0:T(8,128)} collective-permute-done((f32[96,768]{1,0:T(8,128)S(1)}, f32[96,768]{1,0:T(8,128)}, u32[]{:S(2)}, u32[]{:S(2)}) %collective-permute-start.3) | collective-permute-done | bytes 294944 | tf_op jit(solution)/shard_map/ppermute | solution.py:54
  85.9 1.9 maximum_select_fusion.2
  89.0 11.0 %collective-permute-done.4 = f32[192,768]{1,0:T(8,128)} collective-permute-done((f32[192,768]{1,0:T(8,128)}, f32[192,768]{1,0:T(8,128)}, u32[]{:S(2)}, u32[]{:S(2)}) %collective-permute-start.4) | collective-permute-done | bytes 589856 | tf_op jit(solution)/shard_map/ppermute | solution.py:54
  100.0 2.9 %maximum_select_fusion.1 = f32[384,768]{1,0:T(8,128)} fusion(f32[192,768]{1,0:T(8,128)} %maximum_select_fusion.2, f32[192,768]{1,0:T(8,128)} %collective-permute-done.4, pred[]{:T(512)S(6)} %eq.30), kind=kLoop, calls=%fused_computation.23 | loop fusion | flops 884736 | bytes 2359297 | tf_op jit(solution)/shard_map/jit(_where)/select_n | solution.py:55
  102.9 3.8 %collective-permute-start.5 = (f32[384,768]{1,0:T(8,128)}, f32[384,768]{1,0:T(8,128)}, u32[]{:S(2)}, u32[]{:S(2)}) collective-permute-start(f32[384,768]{1,0:T(8,128)} %maximum_select_fusion.1), channel_id=1, source_target_pairs={{0,16},{16,0},{32,48},{48,32},{64,80},{80,64},{96,112},{112,96},{1... | collective-permute-start | bytes 3538952 | tf_op jit(solution)/shard_map/ppermute | solution.py:54
  106.7 2.8 %collective-permute-done.5 = f32[384,768]{1,0:T(8,128)} collective-permute-done((f32[384,768]{1,0:T(8,128)}, f32[384,768]{1,0:T(8,128)}, u32[]{:S(2)}, u32[]{:S(2)}) %collective-permute-start.5) | collective-permute-done | bytes 1179680 | tf_op jit(solution)/shard_map/ppermute | solution.py:54
  109.5 3.1 %select_reduce_fusion = f32[]{:T(128)} fusion(f32[384,768]{1,0:T(8,128)} %collective-permute-done.5, f32[384,768]{1,0:T(8,128)} %maximum_select_fusion.1, pred[]{:T(512)S(6)} %eq.29), kind=kLoop, calls=%fused_computation.9 | loop fusion | flops 3538943 | bytes 2359301 | tf_op jit(solution)/shard_map/reduce_sum | solution.py:92
  113.4 9.3 %multiply_add_fusion.1 = f32[768,768]{1,0:T(8,128)S(1)} fusion(f32[]{:T(128)S(6)} %mul.130, f32[]{:T(128)S(6)} %mul.126, f32[384,768]{1,0:T(8,128)} %collective-permute-done.5, f32[384,768]{1,0:T(8,128)} %maximum_select_fusion.1, pred[]{:T(512)S(6)} %eq.29), kind=kOutput, calls=%fused_computation.8 | convolution fusion | flops 2723217408 | bytes 4718601 | tf_op jit(solution)/shard_map/dot_general | solution.py:23
  122.6 5.5 %fusion.11 = f32[768,768]{1,0:T(8,128)S(1)} fusion(f32[768,768]{1,0:T(8,128)S(1)} %multiply_add_fusion.1, f32[384,768]{1,0:T(8,128)} %maximum_select_fusion.1, f32[384,768]{1,0:T(8,128)} %collective-permute-done.5, pred[]{:T(512)S(6)} %eq.29), kind=kOutput, calls=%fused_computation.16 | convolution fusion | flops 2721447936 | bytes 7077889 | tf_op jit(solution)/shard_map/dot_general | solution.py:23
  128.2 3.1 %fusion.10 = f32[768,768]{1,0:T(8,128)S(1)} fusion(f32[768,768]{1,0:T(8,128)S(1)} %fusion.11, f32[768,768]{1,0:T(8,128)S(1)} %multiply_add_fusion.1), kind=kOutput, calls=%fused_computation.15 | convolution fusion | flops 2719678464 | bytes 7077888 | tf_op jit(solution)/shard_map/dot_general | solution.py:23
  133.9 3.5 %multiply_add_fusion = f32[768,768]{1,0:T(8,128)S(1)} fusion(f32[768,768]{1,0:T(8,128)S(1)} %fusion.10, f32[]{:T(128)S(6)} %div.40), kind=kOutput, calls=%fused_computation.7 | convolution fusion | flops 2720858112 | bytes 4718596 | tf_op jit(solution)/shard_map/dot_general | solution.py:23
  137.4 3.2 %fusion.4 = f32[768,768]{1,0:T(8,128)S(1)} fusion(f32[768,768]{1,0:T(8,128)S(1)} %fusion.10, f32[768,768]{1,0:T(8,128)S(1)} %multiply_add_fusion, f32[]{:T(128)S(6)} %div.40), kind=kOutput, calls=%fused_computation.11 | convolution fusion | flops 2720268288 | bytes 7077892 | tf_op jit(solution)/shard_map/dot_general | solution.py:23
  140.6 3.2 %fusion.12 = f32[768,768]{1,0:T(8,128)S(1)} fusion(f32[768,768]{1,0:T(8,128)S(1)} %fusion.4, f32[768,768]{1,0:T(8,128)S(1)} %multiply_add_fusion), kind=kOutput, calls=%fused_computation.17 | convolution fusion | flops 2719678464 | bytes 7077888 | tf_op jit(solution)/shard_map/dot_general | solution.py:23
  145.1 3.1 %fusion.44 = f32[768,768]{1,0:T(8,128)S(1)} fusion(f32[768,768]{1,0:T(8,128)S(1)} %fusion.12), kind=kOutput, calls=%fused_computation.68 | convolution fusion | flops 2717908992 | bytes 4718592 | tf_op jit(solution)/shard_map/dot_general | solution.py:23
  148.3 1.4 fusion.16
  150.5 2.7 %collective-permute-start.6 = (f32[80,768]{1,0:T(8,128)}, f32[80,768]{1,0:T(8,128)}, u32[]{:S(2)}, u32[]{:S(2)}) collective-permute-start(f32[80,768]{1,0:T(8,128)} %slice.20), channel_id=1, source_target_pairs={{0,1},{2,3},{4,5},{6,7},{8,9},{10,11},{12,13},{14,15},{16,17},{18,... | collective-permute-start | bytes 737288 | tf_op jit(solution)/shard_map/ppermute | solution.py:121
  154.0 3.8 %collective-permute-done.6 = f32[80,768]{1,0:T(8,128)} collective-permute-done((f32[80,768]{1,0:T(8,128)}, f32[80,768]{1,0:T(8,128)}, u32[]{:S(2)}, u32[]{:S(2)}) %collective-permute-start.6) | collective-permute-done | bytes 245792 | tf_op jit(solution)/shard_map/ppermute | solution.py:121
  157.7 2.1 slice_select_fusion
  159.8 71.9 %all-gather.2.cloned.1.call-done = f32[2816,768]{1,0:T(8,128)} async-done(((f32[176,768]{1,0:T(8,128)}), f32[2816,768]{1,0:T(8,128)}) %all-gather.2.cloned.1.call-update) | async-done | bytes 8650768 | tf_op jit(solution)/shard_map/all_gather | solution.py:125
  231.7 3.2 %slice.23 = f32[8,96,768]{2,1,0:T(8,128)} slice(f32[8,352,768]{2,1,0:T(8,128)} %bitcast.25), slice={[0:8], [256:352], [0:768]} | slice | bytes 4718592 | tf_op jit(solution)/shard_map/slice | solution.py:128
  234.9 5.9 %slice.24 = f32[8,256,768]{2,1,0:T(8,128)} slice(f32[8,352,768]{2,1,0:T(8,128)} %bitcast.26), slice={[0:8], [0:256], [0:768]} | slice | bytes 12582912 | tf_op jit(solution)/shard_map/slice | solution.py:127
  (33 shorter events, 21.8 us)
Async XLA Ops:
  7.2 4.6 %copy-start = (bf16[8,256,768]{2,1,0:T(8,128)(2,1)S(1)}, bf16[8,256,768]{2,1,0:T(8,128)(2,1)}, u32[]{:S(2)}) copy-start(bf16[8,256,768]{2,1,0:T(8,128)(2,1)} %param.5) | copy-start | bytes 9437188
  14.8 21.9 %all-to-all-start = ((f32[16,16,768]{2,1,0:T(8,128)}), f32[16,16,768]{2,1,0:T(8,128)}, u32[]{:S(2)}, u32[]{:S(2)}) async-start(f32[16,16,768]{2,1,0:T(8,128)} %bitcast.28), calls=%async_computation | async-start | bytes 1572864 | tf_op jit(solution)/shard_map/all_to_all | solution.py:86
  23.5 208.2 %all-gather.2.cloned.1.call-start = ((), (), s32[]{:S(2)}) async-start(), calls=%async_computation.1 | async-start | bytes 9191424 | tf_op jit(solution)/shard_map/all_gather | solution.py:125
  39.4 1.4 copy-start.3
  41.9 5.1 %collective-permute-start = (f32[384,768]{1,0:T(8,128)}, f32[384,768]{1,0:T(8,128)}, u32[]{:S(2)}, u32[]{:S(2)}) collective-permute-start(f32[384,768]{1,0:T(8,128)} %constant_dynamic-slice_fusion.2), channel_id=1, source_target_pairs={{0,16},{16,0},{32,48},{48,32},{64,80},{80,64},{96,112},{112,96},{1... | collective-permute-start | bytes 3538952 | tf_op jit(solution)/shard_map/ppermute | solution.py:49
  48.7 1.0 copy-start.2
  50.6 14.8 %collective-permute-start.1 = (f32[192,768]{1,0:T(8,128)}, f32[192,768]{1,0:T(8,128)}, u32[]{:S(2)}, u32[]{:S(2)}) collective-permute-start(f32[192,768]{1,0:T(8,128)} %constant_dynamic-slice_fusion.1), channel_id=1, source_target_pairs={{0,32},{16,48},{32,0},{48,16},{64,96},{80,112},{96,64},{112,80},{1... | collective-permute-start | bytes 1769480 | tf_op jit(solution)/shard_map/ppermute | solution.py:49
  66.7 0.8 copy-start.4
  67.6 9.0 %collective-permute-start.2 = (f32[96,768]{1,0:T(8,128)S(1)}, f32[96,768]{1,0:T(8,128)}, u32[]{:S(2)}, u32[]{:S(2)}) collective-permute-start(f32[96,768]{1,0:T(8,128)S(1)} %constant_dynamic-slice_fusion), channel_id=1, source_target_pairs={{0,64},{16,80},{32,96},{48,112},{64,0},{80,16},{96,32},{112,48},{1... | collective-permute-start | bytes 884744 | tf_op jit(solution)/shard_map/ppermute | solution.py:49
  77.7 8.2 %collective-permute-start.3 = (f32[96,768]{1,0:T(8,128)S(1)}, f32[96,768]{1,0:T(8,128)}, u32[]{:S(2)}, u32[]{:S(2)}) collective-permute-start(f32[96,768]{1,0:T(8,128)S(1)} %dynamic-slice_add_fusion.2), channel_id=1, source_target_pairs={{0,64},{16,80},{32,96},{48,112},{64,0},{80,16},{96,32},{112,48},{1... | collective-permute-start | bytes 884744 | tf_op jit(solution)/shard_map/ppermute | solution.py:54
  87.8 12.3 %collective-permute-start.4 = (f32[192,768]{1,0:T(8,128)}, f32[192,768]{1,0:T(8,128)}, u32[]{:S(2)}, u32[]{:S(2)}) collective-permute-start(f32[192,768]{1,0:T(8,128)} %maximum_select_fusion.2), channel_id=1, source_target_pairs={{0,32},{16,48},{32,0},{48,16},{64,96},{80,112},{96,64},{112,80},{1... | collective-permute-start | bytes 1769480 | tf_op jit(solution)/shard_map/ppermute | solution.py:54
  102.9 6.6 %collective-permute-start.5 = (f32[384,768]{1,0:T(8,128)}, f32[384,768]{1,0:T(8,128)}, u32[]{:S(2)}, u32[]{:S(2)}) collective-permute-start(f32[384,768]{1,0:T(8,128)} %maximum_select_fusion.1), channel_id=1, source_target_pairs={{0,16},{16,0},{32,48},{48,32},{64,80},{80,64},{96,112},{112,96},{1... | collective-permute-start | bytes 3538952 | tf_op jit(solution)/shard_map/ppermute | solution.py:54
  149.7 3.5 %copy-start.1 = (f32[256,768]{1,0:T(8,128)}, f32[256,768]{1,0:T(8,128)S(1)}, u32[]{:S(2)}) copy-start(f32[256,768]{1,0:T(8,128)S(1)} %fusion.16) | copy-start | bytes 2359300
  150.5 7.3 %collective-permute-start.6 = (f32[80,768]{1,0:T(8,128)}, f32[80,768]{1,0:T(8,128)}, u32[]{:S(2)}, u32[]{:S(2)}) collective-permute-start(f32[80,768]{1,0:T(8,128)} %slice.20), channel_id=1, source_target_pairs={{0,1},{2,3},{4,5},{6,7},{8,9},{10,11},{12,13},{14,15},{16,17},{18,... | collective-permute-start | bytes 737288 | tf_op jit(solution)/shard_map/ppermute | solution.py:121
Sparse Core Ops, SparseCore 0:
  159.9 71.6 all-gather.1

commit v8 on v6

--- a/solution.py
+++ b/solution.py
@@ -66,18 +66,21 @@
     denom = jnp.sqrt(total) + epsilon
     current = rows / denom
     shrink = 1.0 / (denom * denom)
-    for iteration in range(ITERS):
+    for iteration in range(ITERS - 1):
         square_gram = dot(gram, gram)
         if iteration == 0:
             mixer = (coef_b * shrink) * gram + (coef_c * shrink * shrink) * square_gram
         else:
             mixer = coef_b * gram + coef_c * square_gram
         current = coef_a * current + dot(current, mixer)
-        if iteration + 1 < ITERS:
-            full = mixer + coef_a * eye
-            gram = dot(full, dot(gram, full))
-            if iteration == 0:
-                gram = shrink * gram
+        full = mixer + coef_a * eye
+        gram = dot(full, dot(gram, full))
+        if iteration == 0:
+            gram = shrink * gram
+    if ITERS == 1:
+        gram = shrink * gram
+    side = dot(current, gram)
+    current = coef_a * current + (coef_b * side + coef_c * dot(side, gram))
 
     is_square = member % 2 == 1
     scale = jnp.where(

time: 238 us -> 236 us (level)
  no operation moved by 1% of the time
where the time goes in v8:
time: 236 us
  waiting for transfers between devices  141 us (60%)
  matrix products  30.7 us (13%)
  blocking collectives  21.9 us (9%)
  between operations  15 us (6%)
  local copies, waits for them, and re-layouts  13.7 us (6%)
  other arithmetic  9.22 us (4%)
  starting transfers between devices  4.06 us (2%)
    all_gather x1, waiting for transfers between devices, shards(): gathered = lax.all_gather(mine, 'tensor', axis=0, tiled=True)  76.3 us
    psum x1, waiting for transfers between devices, shards(): gram = lax.psum(gram_of(rows), 'shard')  63.1 us
    dot_general x10, matrix products, dot(): jnp.dot(x, y, precision=PRECISION, preferred_element_type=jnp.float32)  28.1 us
    all_to_all x1, blocking collectives, shards(): lax.all_to_all(send, 'tensor', split_axis=0, concat_axis=0, tiled=True)  21.9 us
    slice x1, local copies, waits for them, and re-layouts, shards(): update_wide = gathered[:, :wide_rows]  5.94 us
  transfers between devices with their start and end apart: 3, of which 3 were waited for; matrix products, arithmetic and copies ran while one was open for 0% of the time, Pallas kernels for 0%

profile of v8, /device:TPU:1, one launch (start us, length us, event | category | flops | bytes accessed | tf_op | source)
XLA Modules:
  0.0 235.9 jit_solution(12891681526562934058)
XLA Ops:
  7.2 1.1 broadcast_multiply_fusion.1
  8.3 1.0 constant_dynamic-slice_fusion
  9.3 0.7 convert_add_fusion.3
  10.0 0.8 pad_bitcast_fusion
  10.7 1.0 broadcast_multiply_fusion
  11.8 0.9 convert_add_fusion.1
  12.7 1.0 pad_maximum_fusion
  13.7 0.3 copy.13
  14.0 21.9 %all_to_all.5 = f32[16,16,768]{2,1,0:T(8,128)S(1)} all-to-all(f32[16,16,768]{2,1,0:T(8,128)S(1)} %bitcast.32), channel_id=1, replica_groups=mesh['shard'=8,'tensor'=16] {'tensor'}, dimensions={0} | all-to-all | bytes 1572864 | tf_op jit(solution)/shard_map/all_to_all | solution.py:59
  35.9 0.9 copy-done.3
  36.8 2.7 %convolution_bitcast_fusion = f32[768,768]{1,0:T(8,128)} fusion(f32[16,16,768]{2,1,0:T(8,128)S(1)} %all_to_all.5), kind=kOutput, calls=%fused_computation.13 | convolution fusion | flops 905969664 | bytes 3145728 | tf_op jit(solution)/shard_map/dot_general | solution.py:27
  39.5 0.2 all-gather.2.cloned.1.call-start
  39.7 63.1 %all-reduce.3.cloned.1.call-done = f32[768,768]{1,0:T(8,128)} async-done(((f32[768,768]{1,0:T(8,128)}), f32[768,768]{1,0:T(8,128)}) %all-reduce.3.cloned.1.call-update) | async-done | bytes 2359312 | tf_op jit(solution)/shard_map/psum | solution.py:62
  102.8 2.4 %select_reduce_fusion = f32[]{:T(128)} fusion(f32[768,768]{1,0:T(8,128)} %all-reduce.3.cloned.1.call-done), kind=kLoop, calls=%fused_computation.4 | loop fusion | flops 1769471 | bytes 2359300 | tf_op jit(solution)/shard_map/reduce_sum | solution.py:65
  105.9 6.3 %multiply_add_fusion.1 = f32[768,768]{1,0:T(8,128)S(1)} fusion(f32[768,768]{1,0:T(8,128)} %all-reduce.3.cloned.1.call-done, f32[]{:T(128)S(6)} %mul.118, f32[]{:T(128)S(6)} %mul.114), kind=kOutput, calls=%fused_computation.3 | convolution fusion | flops 2719678464 | bytes 4718600 | tf_op jit(solution)/shard_map/dot_general | solution.py:23
  112.3 3.1 %fusion.7 = f32[768,768]{1,0:T(8,128)S(1)} fusion(f32[768,768]{1,0:T(8,128)S(1)} %copy-done.1, f32[768,768]{1,0:T(8,128)S(1)} %multiply_add_fusion.1), kind=kOutput, calls=%fused_computation.11 | convolution fusion | flops 2719678464 | bytes 7077888 | tf_op jit(solution)/shard_map/dot_general | solution.py:23
  115.4 3.2 %fusion.6 = f32[768,768]{1,0:T(8,128)S(1)} fusion(f32[768,768]{1,0:T(8,128)S(1)} %fusion.7, f32[768,768]{1,0:T(8,128)S(1)} %multiply_add_fusion.1), kind=kOutput, calls=%fused_computation.10 | convolution fusion | flops 2719678464 | bytes 7077888 | tf_op jit(solution)/shard_map/dot_general | solution.py:23
  118.7 1.4 convolution_add_fusion.1
  120.1 3.5 %multiply_add_fusion = f32[768,768]{1,0:T(8,128)S(1)} fusion(f32[768,768]{1,0:T(8,128)S(1)} %fusion.6, f32[]{:T(128)S(6)} %div.15), kind=kOutput, calls=%fused_computation.2 | convolution fusion | flops 2720858112 | bytes 4718596 | tf_op jit(solution)/shard_map/dot_general | solution.py:23
  123.6 3.2 %fusion = f32[768,768]{1,0:T(8,128)S(1)} fusion(f32[768,768]{1,0:T(8,128)S(1)} %fusion.6, f32[768,768]{1,0:T(8,128)S(1)} %multiply_add_fusion, f32[]{:T(128)S(6)} %div.15), kind=kOutput, calls=%fused_computation.6 | convolution fusion | flops 2720268288 | bytes 7077892 | tf_op jit(solution)/shard_map/dot_general | solution.py:23
  126.8 3.2 %fusion.8 = f32[768,768]{1,0:T(8,128)S(1)} fusion(f32[768,768]{1,0:T(8,128)S(1)} %fusion, f32[768,768]{1,0:T(8,128)S(1)} %multiply_add_fusion), kind=kOutput, calls=%fused_computation.12 | convolution fusion | flops 2719678464 | bytes 7077888 | tf_op jit(solution)/shard_map/dot_general | solution.py:23
  129.9 1.4 convolution_add_fusion
  131.3 1.4 fusion.31
  132.7 1.5 fusion.11
  134.2 0.8 slice.20
  135.0 3.8 %collective-permute-start = (f32[80,768]{1,0:T(8,128)}, f32[80,768]{1,0:T(8,128)}, u32[]{:S(2)}, u32[]{:S(2)}) collective-permute-start(f32[80,768]{1,0:T(8,128)} %slice.20), channel_id=1, source_target_pairs={{0,1},{2,3},{4,5},{6,7},{8,9},{10,11},{12,13},{14,15},{16,17},{18,... | collective-permute-start | bytes 737288 | tf_op jit(solution)/shard_map/ppermute | solution.py:97
  138.8 0.8 reshape.37
  139.6 1.9 collective-permute-done
  141.5 2.1 slice_select_fusion
  143.6 76.3 %all-gather.2.cloned.1.call-done = f32[2816,768]{1,0:T(8,128)} async-done(((f32[176,768]{1,0:T(8,128)}), f32[2816,768]{1,0:T(8,128)}) %all-gather.2.cloned.1.call-update) | async-done | bytes 8650768 | tf_op jit(solution)/shard_map/all_gather | solution.py:101
  219.9 3.2 %slice.23 = f32[8,96,768]{2,1,0:T(8,128)} slice(f32[8,352,768]{2,1,0:T(8,128)} %bitcast.29), slice={[0:8], [256:352], [0:768]} | slice | bytes 4718592 | tf_op jit(solution)/shard_map/slice | solution.py:104
  223.1 5.9 %slice.24 = f32[8,256,768]{2,1,0:T(8,128)} slice(f32[8,352,768]{2,1,0:T(8,128)} %bitcast.30), slice={[0:8], [0:256], [0:768]} | slice | bytes 12582912 | tf_op jit(solution)/shard_map/slice | solution.py:103
  (15 shorter events, 0.2 us)
Async XLA Ops:
  7.2 4.6 %copy-start = (bf16[8,256,768]{2,1,0:T(8,128)(2,1)S(1)}, bf16[8,256,768]{2,1,0:T(8,128)(2,1)}, u32[]{:S(2)}) copy-start(bf16[8,256,768]{2,1,0:T(8,128)(2,1)} %param.5) | copy-start | bytes 9437188
  7.2 95.6 %all-reduce.3.cloned.1.call-start = ((), (), s32[]{:S(2)}) async-start(), calls=%async_computation.1 | async-start | bytes 4718592 | tf_op jit(solution)/shard_map/psum | solution.py:62
  35.9 0.9 copy-start.3
  39.5 180.4 %all-gather.2.cloned.1.call-start = ((), (), s32[]{:S(2)}) async-start(), calls=%async_computation.2 | async-start | bytes 9191424 | tf_op jit(solution)/shard_map/all_gather | solution.py:101
  105.9 6.4 %copy-start.1 = (f32[768,768]{1,0:T(8,128)S(1)}, f32[768,768]{1,0:T(8,128)}, u32[]{:S(2)}) copy-start(f32[768,768]{1,0:T(8,128)} %all-reduce.3.cloned.1.call-done) | copy-start | bytes 7077892
  115.4 3.2 %copy-start.4 = (f32[16,16,768]{2,1,0:T(8,128)S(1)}, f32[16,16,768]{2,1,0:T(8,128)}, u32[]{:S(2)}) copy-start(f32[16,16,768]{2,1,0:T(8,128)} %copy-done.3) | copy-start | bytes 2359300
  134.2 4.6 %copy-start.2 = (f32[256,768]{1,0:T(8,128)}, f32[256,768]{1,0:T(8,128)S(1)}, u32[]{:S(2)}) copy-start(f32[256,768]{1,0:T(8,128)S(1)} %fusion.11) | copy-start | bytes 2359300
  135.0 6.5 %collective-permute-start = (f32[80,768]{1,0:T(8,128)}, f32[80,768]{1,0:T(8,128)}, u32[]{:S(2)}, u32[]{:S(2)}) collective-permute-start(f32[80,768]{1,0:T(8,128)} %slice.20), channel_id=1, source_target_pairs={{0,1},{2,3},{4,5},{6,7},{8,9},{10,11},{12,13},{14,15},{16,17},{18,... | collective-permute-start | bytes 737288 | tf_op jit(solution)/shard_map/ppermute | solution.py:97
Sparse Core Ops, SparseCore 0:
  39.6 63.1 all-reduce.2
  143.7 76.1 all-gather.1

commit v9 on v8

--- a/solution.py
+++ b/solution.py
@@ -65,38 +65,35 @@
     total = jnp.sum(gram * eye)
     denom = jnp.sqrt(total) + epsilon
     current = rows / denom
-    shrink = 1.0 / (denom * denom)
+    gram = lax.optimization_barrier(gram / (denom * denom))
     for iteration in range(ITERS - 1):
         square_gram = dot(gram, gram)
-        if iteration == 0:
-            mixer = (coef_b * shrink) * gram + (coef_c * shrink * shrink) * square_gram
-        else:
-            mixer = coef_b * gram + coef_c * square_gram
+        mixer = coef_b * gram + coef_c * square_gram
         current = coef_a * current + dot(current, mixer)
         full = mixer + coef_a * eye
         gram = dot(full, dot(gram, full))
-        if iteration == 0:
-            gram = shrink * gram
-    if ITERS == 1:
-        gram = shrink * gram
-    side = dot(current, gram)
-    current = coef_a * current + (coef_b * side + coef_c * dot(side, gram))
-
     is_square = member % 2 == 1
     scale = jnp.where(
         is_square, jnp.float32(math.sqrt(D)), jnp.float32(math.sqrt(FF))
     )
-    update = scale * current
+
+    def finish(block):
+        side = dot(block, gram)
+        return scale * (coef_a * block + (coef_b * side + coef_c * dot(side, gram)))
+
     square_piece = piece - pad
+    split = (current.shape[0] + (piece - pad) * tensor_count) // 2
+    head, tail = finish(current[:split]), finish(current[split:])
+    update = jnp.concatenate([head, tail], axis=0)
     square_rows = update.reshape(tensor_count, piece, -1)[:, :square_piece]
     square_rows = square_rows.reshape(tensor_count * square_piece, -1)
     wide_rows = update.shape[0]
     chunk = (square_rows.shape[0] + wide_rows) // 2
-    assert 2 * chunk == square_rows.shape[0] + wide_rows
+    assert 2 * chunk == square_rows.shape[0] + wide_rows and chunk == split
     to_odd = [(2 * j, 2 * j + 1) for j in range(count_square)]
-    handed = lax.ppermute(update[chunk:], "tensor", to_odd)
+    handed = lax.ppermute(tail, "tensor", to_odd)
     mine = jnp.where(
-        is_square, jnp.concatenate([handed, square_rows], axis=0), update[:chunk]
+        is_square, jnp.concatenate([handed, square_rows], axis=0), head
     )
     gathered = lax.all_gather(mine, "tensor", axis=0, tiled=True)
     gathered = gathered.reshape(count_square, 2 * chunk, update.shape[1])

time: 236 us -> 235 us (level)
  waiting for transfers between devices: 141 us -> 138 us
  other arithmetic: 9.22 us -> 12 us
    dot_general x10 -> x12, matrix products: 28.1 us -> 27 us  [dot(): jnp.dot(x, y, precision=PRECISION, preferred_element_type=jnp.float32)]
  transfers between devices with their start and end apart: 3 -> 3, of which waited for: 3 -> 2; matrix products, arithmetic and copies ran while one was open for 0% -> 1% of each run, Pallas kernels for 0% -> 0%
where the time goes in v9:
time: 235 us; the launch traced here: 234 us
  waiting for transfers between devices  138 us (59%)
  matrix products  29.6 us (13%)
  blocking collectives  21.9 us (9%)
  between operations  14.9 us (6%)
  local copies, waits for them, and re-layouts  13.7 us (6%)
  other arithmetic  12 us (5%)
  starting transfers between devices  4.06 us (2%)
    all_gather x1, waiting for transfers between devices, shards(): gathered = lax.all_gather(mine, 'tensor', axis=0, tiled=True)  75.1 us
    psum x1, waiting for transfers between devices, shards(): gram = lax.psum(gram_of(rows), 'shard')  63.1 us
    dot_general x12, matrix products, dot(): jnp.dot(x, y, precision=PRECISION, preferred_element_type=jnp.float32)  27 us
    all_to_all x1, blocking collectives, shards(): lax.all_to_all(send, 'tensor', split_axis=0, concat_axis=0, tiled=True)  21.9 us
    slice x1, local copies, waits for them, and re-layouts, shards(): update_wide = gathered[:, :wide_rows]  5.94 us
  transfers between devices with their start and end apart: 3, of which 2 were waited for; matrix products, arithmetic and copies ran while one was open for 1% of the time, Pallas kernels for 0%

profile of v9, /device:TPU:1, one launch (start us, length us, event | category | flops | bytes accessed | tf_op | source)
XLA Modules:
  0.0 234.5 jit_solution(11119530190702908651)
XLA Ops:
  7.2 1.1 broadcast_multiply_fusion.1
  8.3 1.0 constant_dynamic-slice_fusion
  10.0 0.8 pad_bitcast_fusion
  10.7 1.0 broadcast_multiply_fusion
  11.8 0.9 convert_add_fusion.1
  12.7 1.0 pad_maximum_fusion
  14.0 21.9 %all_to_all.5 = f32[16,16,768]{2,1,0:T(8,128)S(1)} all-to-all(f32[16,16,768]{2,1,0:T(8,128)S(1)} %bitcast.36), channel_id=1, replica_groups=mesh['shard'=8,'tensor'=16] {'tensor'}, dimensions={0} | all-to-all | bytes 1572864 | tf_op jit(solution)/shard_map/all_to_all | solution.py:59
  35.9 0.9 copy-done.2
  36.8 2.7 %convolution_bitcast_fusion = f32[768,768]{1,0:T(8,128)} fusion(f32[16,16,768]{2,1,0:T(8,128)S(1)} %all_to_all.5), kind=kOutput, calls=%fused_computation.10 | convolution fusion | flops 905969664 | bytes 3145728 | tf_op jit(solution)/shard_map/dot_general | solution.py:27
  39.7 63.1 %all-reduce.3.cloned.1.call-done = f32[768,768]{1,0:T(8,128)} async-done(((f32[768,768]{1,0:T(8,128)}), f32[768,768]{1,0:T(8,128)}) %all-reduce.3.cloned.1.call-update) | async-done | bytes 2359312 | tf_op jit(solution)/shard_map/psum | solution.py:62
  102.8 2.4 %select_reduce_fusion = f32[]{:T(128)} fusion(f32[768,768]{1,0:T(8,128)} %all-reduce.3.cloned.1.call-done), kind=kLoop, calls=%fused_computation.4 | loop fusion | flops 1769471 | bytes 2359300 | tf_op jit(solution)/shard_map/reduce_sum | solution.py:65
  105.9 1.8 broadcast_divide_fusion
  107.7 3.3 %multiply_add_fusion.1 = f32[768,768]{1,0:T(8,128)S(1)} fusion(f32[768,768]{1,0:T(8,128)S(1)} %broadcast_divide_fusion), kind=kOutput, calls=%fused_computation.3 | convolution fusion | flops 2719678464 | bytes 4718592 | tf_op jit(solution)/shard_map/dot_general | solution.py:23
  111.0 3.1 %fusion.1 = f32[768,768]{1,0:T(8,128)S(1)} fusion(f32[768,768]{1,0:T(8,128)S(1)} %broadcast_divide_fusion, f32[768,768]{1,0:T(8,128)S(1)} %multiply_add_fusion.1), kind=kOutput, calls=%fused_computation.7 | convolution fusion | flops 2719678464 | bytes 7077888 | tf_op jit(solution)/shard_map/dot_general | solution.py:23
  114.1 3.2 %fusion = f32[768,768]{1,0:T(8,128)S(1)} fusion(f32[768,768]{1,0:T(8,128)S(1)} %fusion.1, f32[768,768]{1,0:T(8,128)S(1)} %multiply_add_fusion.1), kind=kOutput, calls=%fused_computation.6 | convolution fusion | flops 2719678464 | bytes 7077888 | tf_op jit(solution)/shard_map/dot_general | solution.py:23
  117.4 1.4 convolution_add_fusion.1
  118.8 3.5 %multiply_add_fusion = f32[768,768]{1,0:T(8,128)S(1)} fusion(f32[768,768]{1,0:T(8,128)S(1)} %fusion), kind=kOutput, calls=%fused_computation.2 | convolution fusion | flops 2719678464 | bytes 4718592 | tf_op jit(solution)/shard_map/dot_general | solution.py:23
  122.3 3.1 %fusion.3 = f32[768,768]{1,0:T(8,128)S(1)} fusion(f32[768,768]{1,0:T(8,128)S(1)} %fusion, f32[768,768]{1,0:T(8,128)S(1)} %multiply_add_fusion), kind=kOutput, calls=%fused_computation.9 | convolution fusion | flops 2719678464 | bytes 7077888 | tf_op jit(solution)/shard_map/dot_general | solution.py:23
  125.5 1.4 convolution_add_fusion
  126.9 3.2 %fusion.2 = f32[768,768]{1,0:T(8,128)S(1)} fusion(f32[768,768]{1,0:T(8,128)S(1)} %fusion.3, f32[768,768]{1,0:T(8,128)S(1)} %multiply_add_fusion), kind=kOutput, calls=%fused_computation.8 | convolution fusion | flops 2719678464 | bytes 7077888 | tf_op jit(solution)/shard_map/dot_general | solution.py:23
  130.1 0.9 fusion.21
  131.0 1.1 fusion.18
  132.1 1.6 fusion.17
  133.7 3.8 %collective-permute-start = (f32[80,768]{1,0:T(8,128)}, f32[80,768]{1,0:T(8,128)}, u32[]{:S(2)}, u32[]{:S(2)}) collective-permute-start(f32[80,768]{1,0:T(8,128)} %fusion.17), channel_id=1, source_target_pairs={{0,1},{2,3},{4,5},{6,7},{8,9},{10,11},{12,13},{14,15},{16,17},{18,... | collective-permute-start | bytes 737288 | tf_op jit(solution)/shard_map/ppermute | solution.py:94
  137.5 1.2 fusion.6
  138.7 0.8 copy-done.1
  139.5 1.0 pad_maximum_fusion.1
  140.5 0.8 reshape.37
  141.3 2.1 maximum_select_fusion
  143.3 75.1 %all-gather.2.cloned.1.call-done = f32[2816,768]{1,0:T(8,128)} async-done(((f32[176,768]{1,0:T(8,128)}), f32[2816,768]{1,0:T(8,128)}) %all-gather.2.cloned.1.call-update) | async-done | bytes 8650768 | tf_op jit(solution)/shard_map/all_gather | solution.py:98
  218.5 3.2 %slice.23 = f32[8,96,768]{2,1,0:T(8,128)} slice(f32[8,352,768]{2,1,0:T(8,128)} %bitcast.34), slice={[0:8], [256:352], [0:768]} | slice | bytes 4718592 | tf_op jit(solution)/shard_map/slice | solution.py:101
  221.7 5.9 %slice.24 = f32[8,256,768]{2,1,0:T(8,128)} slice(f32[8,352,768]{2,1,0:T(8,128)} %bitcast.35), slice={[0:8], [0:256], [0:768]} | slice | bytes 12582912 | tf_op jit(solution)/shard_map/slice | solution.py:100
  (16 shorter events, 1.4 us)
Async XLA Ops:
  7.2 4.6 %copy-start = (bf16[8,256,768]{2,1,0:T(8,128)(2,1)S(1)}, bf16[8,256,768]{2,1,0:T(8,128)(2,1)}, u32[]{:S(2)}) copy-start(bf16[8,256,768]{2,1,0:T(8,128)(2,1)} %param.5) | copy-start | bytes 9437188
  7.2 95.6 %all-reduce.3.cloned.1.call-start = ((), (), s32[]{:S(2)}) async-start(), calls=%async_computation.1 | async-start | bytes 4718592 | tf_op jit(solution)/shard_map/psum | solution.py:62
  35.9 0.9 copy-start.2
  39.5 179.0 %all-gather.2.cloned.1.call-start = ((), (), s32[]{:S(2)}) async-start(), calls=%async_computation.2 | async-start | bytes 9191424 | tf_op jit(solution)/shard_map/all_gather | solution.py:98
  114.1 3.2 %copy-start.3 = (f32[16,16,768]{2,1,0:T(8,128)S(1)}, f32[16,16,768]{2,1,0:T(8,128)}, u32[]{:S(2)}) copy-start(f32[16,16,768]{2,1,0:T(8,128)} %copy-done.2) | copy-start | bytes 2359300
  133.7 7.6 %collective-permute-start = (f32[80,768]{1,0:T(8,128)}, f32[80,768]{1,0:T(8,128)}, u32[]{:S(2)}, u32[]{:S(2)}) collective-permute-start(f32[80,768]{1,0:T(8,128)} %fusion.17), channel_id=1, source_target_pairs={{0,1},{2,3},{4,5},{6,7},{8,9},{10,11},{12,13},{14,15},{16,17},{18,... | collective-permute-start | bytes 737288 | tf_op jit(solution)/shard_map/ppermute | solution.py:94
  138.7 0.8 copy-start.1
Sparse Core Ops, SparseCore 0:
  39.6 63.1 all-reduce.2
  143.5 74.9 all-gather.1

commit v10 on v9

--- a/solution.py
+++ b/solution.py
@@ -52,8 +52,8 @@
 
     piece = look_wide.shape[1]
     pad = piece - look_square.shape[1]
-    padded_square = jnp.pad(look_square, ((0, 0), (0, pad), (0, 0)))
-    send = jnp.stack([look_wide, padded_square], axis=1).reshape(
+    zeros = jnp.zeros((count_square, pad, look_wide.shape[2]), jnp.float32)
+    send = jnp.concatenate([look_wide, look_square, zeros], axis=1).reshape(
         tensor_count, piece, look_wide.shape[2]
     )
     held = lax.all_to_all(send, "tensor", split_axis=0, concat_axis=0, tiled=True)

time: 235 us -> 230 us (0.979)
  other arithmetic: 12 us -> 8.35 us
  transfers between devices with their start and end apart: 3 -> 3, of which waited for: 2 -> 3; matrix products, arithmetic and copies ran while one was open for 1% -> 1% of each run, Pallas kernels for 0% -> 0%
where the time goes in v10:
time: 230 us; the launch traced here: 229 us
  waiting for transfers between devices  140 us (61%)
  matrix products  28.9 us (13%)
  blocking collectives  21.9 us (10%)
  between operations  15 us (7%)
  local copies, waits for them, and re-layouts  11.5 us (5%)
  other arithmetic  8.35 us (4%)
  starting transfers between devices  3.2 us (1%)
    all_gather x1, waiting for transfers between devices, shards(): gathered = lax.all_gather(mine, 'tensor', axis=0, tiled=True)  75.3 us
    psum x1, waiting for transfers between devices, shards(): gram = lax.psum(gram_of(rows), 'shard')  63.3 us
    dot_general x12, matrix products, dot(): jnp.dot(x, y, precision=PRECISION, preferred_element_type=jnp.float32)  26.2 us
    all_to_all x1, blocking collectives, shards(): lax.all_to_all(send, 'tensor', split_axis=0, concat_axis=0, tiled=True)  21.9 us
    slice x1, local copies, waits for them, and re-layouts, shards(): update_wide = gathered[:, :wide_rows]  5.94 us
  transfers between devices with their start and end apart: 3, of which 3 were waited for; matrix products, arithmetic and copies ran while one was open for 1% of the time, Pallas kernels for 0%

profile of v10, /device:TPU:1, one launch (start us, length us, event | category | flops | bytes accessed | tf_op | source)
XLA Modules:
  0.0 229.3 jit_solution(14798981202441236704)
XLA Ops:
  7.2 1.0 broadcast_multiply_fusion.1
  8.2 0.3 copy-done
  8.6 0.7 convert_add_fusion.3
  9.3 1.0 broadcast_multiply_fusion
  10.4 1.8 fusion.20
  12.2 0.1 maximum_maximum_fusion
  12.4 21.9 %all_to_all.5 = f32[16,16,768]{2,1,0:T(8,128)S(1)} all-to-all(f32[16,16,768]{2,1,0:T(8,128)S(1)} %bitcast.34), channel_id=1, replica_groups=mesh['shard'=8,'tensor'=16] {'tensor'}, dimensions={0} | all-to-all | bytes 1572864 | tf_op jit(solution)/shard_map/all_to_all | solution.py:59
  34.3 0.9 copy-done.2
  35.2 2.7 %convolution_bitcast_fusion = f32[768,768]{1,0:T(8,128)} fusion(f32[16,16,768]{2,1,0:T(8,128)S(1)} %all_to_all.5), kind=kOutput, calls=%fused_computation.10 | convolution fusion | flops 905969664 | bytes 3145728 | tf_op jit(solution)/shard_map/dot_general | solution.py:27
  37.9 63.3 %all-reduce.2.cloned.1.call-done = f32[768,768]{1,0:T(8,128)} async-done(((f32[768,768]{1,0:T(8,128)}), f32[768,768]{1,0:T(8,128)}) %all-reduce.2.cloned.1.call-update) | async-done | bytes 2359312 | tf_op jit(solution)/shard_map/psum | solution.py:62
  101.2 2.5 %select_reduce_fusion = f32[]{:T(128)} fusion(f32[768,768]{1,0:T(8,128)} %all-reduce.2.cloned.1.call-done), kind=kLoop, calls=%fused_computation.4 | loop fusion | flops 1769471 | bytes 2359300 | tf_op jit(solution)/shard_map/reduce_sum | solution.py:65
  104.4 0.2 broadcast_divide_fusion
  104.6 3.3 %multiply_add_fusion.1 = f32[768,768]{1,0:T(8,128)S(1)} fusion(f32[768,768]{1,0:T(8,128)S(1)} %broadcast_divide_fusion), kind=kOutput, calls=%fused_computation.3 | convolution fusion | flops 2719678464 | bytes 4718592 | tf_op jit(solution)/shard_map/dot_general | solution.py:23
  107.9 3.1 %fusion.1 = f32[768,768]{1,0:T(8,128)S(1)} fusion(f32[768,768]{1,0:T(8,128)S(1)} %broadcast_divide_fusion, f32[768,768]{1,0:T(8,128)S(1)} %multiply_add_fusion.1), kind=kOutput, calls=%fused_computation.7 | convolution fusion | flops 2719678464 | bytes 7077888 | tf_op jit(solution)/shard_map/dot_general | solution.py:23
  111.1 3.2 %fusion = f32[768,768]{1,0:T(8,128)S(1)} fusion(f32[768,768]{1,0:T(8,128)S(1)} %fusion.1, f32[768,768]{1,0:T(8,128)S(1)} %multiply_add_fusion.1), kind=kOutput, calls=%fused_computation.6 | convolution fusion | flops 2719678464 | bytes 7077888 | tf_op jit(solution)/shard_map/dot_general | solution.py:23
  114.2 0.1 broadcast_divide_fusion.1
  114.3 1.4 convolution_add_fusion.1
  115.7 3.5 %multiply_add_fusion = f32[768,768]{1,0:T(8,128)S(1)} fusion(f32[768,768]{1,0:T(8,128)S(1)} %fusion), kind=kOutput, calls=%fused_computation.2 | convolution fusion | flops 2719678464 | bytes 4718592 | tf_op jit(solution)/shard_map/dot_general | solution.py:23
  119.2 3.1 %fusion.3 = f32[768,768]{1,0:T(8,128)S(1)} fusion(f32[768,768]{1,0:T(8,128)S(1)} %fusion, f32[768,768]{1,0:T(8,128)S(1)} %multiply_add_fusion), kind=kOutput, calls=%fused_computation.9 | convolution fusion | flops 2719678464 | bytes 7077888 | tf_op jit(solution)/shard_map/dot_general | solution.py:23
  122.4 1.4 convolution_add_fusion
  123.8 3.2 %fusion.2 = f32[768,768]{1,0:T(8,128)S(1)} fusion(f32[768,768]{1,0:T(8,128)S(1)} %fusion.3, f32[768,768]{1,0:T(8,128)S(1)} %multiply_add_fusion), kind=kOutput, calls=%fused_computation.8 | convolution fusion | flops 2719678464 | bytes 7077888 | tf_op jit(solution)/shard_map/dot_general | solution.py:23
  127.0 0.9 fusion.21
  127.9 1.1 fusion.18
  129.0 0.9 fusion.17
  129.9 3.1 %collective-permute-start = (f32[80,768]{1,0:T(8,128)S(1)}, f32[80,768]{1,0:T(8,128)S(1)}, u32[]{:S(2)}, u32[]{:S(2)}) collective-permute-start(f32[80,768]{1,0:T(8,128)S(1)} %fusion.17), channel_id=1, source_target_pairs={{0,1},{2,3},{4,5},{6,7},{8,9},{10,11},{12,13},{14,15},{16,17},{18,... | collective-permute-start | bytes 737288 | tf_op jit(solution)/shard_map/ppermute | solution.py:94
  133.0 1.1 fusion.6
  134.4 1.8 collective-permute-done
  136.2 0.9 maximum_select_fusion
  137.0 1.0 copy.14
  138.0 75.3 %all-gather.2.cloned.1.call-done = f32[2816,768]{1,0:T(8,128)} async-done(((f32[176,768]{1,0:T(8,128)}), f32[2816,768]{1,0:T(8,128)}) %all-gather.2.cloned.1.call-update) | async-done | bytes 8650768 | tf_op jit(solution)/shard_map/all_gather | solution.py:98
  213.3 3.2 %slice.23 = f32[8,96,768]{2,1,0:T(8,128)} slice(f32[8,352,768]{2,1,0:T(8,128)} %bitcast.32), slice={[0:8], [256:352], [0:768]} | slice | bytes 4718592 | tf_op jit(solution)/shard_map/slice | solution.py:101
  216.5 5.9 %slice.24 = f32[8,256,768]{2,1,0:T(8,128)} slice(f32[8,352,768]{2,1,0:T(8,128)} %bitcast.33), slice={[0:8], [0:256], [0:768]} | slice | bytes 12582912 | tf_op jit(solution)/shard_map/slice | solution.py:100
  (19 shorter events, 0.4 us)
Async XLA Ops:
  7.2 1.3 copy-start
  7.2 94.0 %all-reduce.2.cloned.1.call-start = ((), (), s32[]{:S(2)}) async-start(), calls=%async_computation.1 | async-start | bytes 4718592 | tf_op jit(solution)/shard_map/psum | solution.py:62
  34.3 0.9 copy-start.2
  37.9 175.5 %all-gather.2.cloned.1.call-start = ((), (), s32[]{:S(2)}) async-start(), calls=%async_computation.2 | async-start | bytes 9191424 | tf_op jit(solution)/shard_map/all_gather | solution.py:98
  101.2 3.2 %copy-start.1 = (f32[768,768]{1,0:T(8,128)S(1)}, f32[768,768]{1,0:T(8,128)}, u32[]{:S(2)}) copy-start(f32[768,768]{1,0:T(8,128)} %all-reduce.2.cloned.1.call-done) | copy-start | bytes 7077892
  111.1 3.2 %copy-start.3 = (f32[16,16,768]{2,1,0:T(8,128)S(1)}, f32[16,16,768]{2,1,0:T(8,128)}, u32[]{:S(2)}) copy-start(f32[16,16,768]{2,1,0:T(8,128)} %copy-done.2) | copy-start | bytes 2359300
  129.9 6.2 %collective-permute-start = (f32[80,768]{1,0:T(8,128)S(1)}, f32[80,768]{1,0:T(8,128)S(1)}, u32[]{:S(2)}, u32[]{:S(2)}) collective-permute-start(f32[80,768]{1,0:T(8,128)S(1)} %fusion.17), channel_id=1, source_target_pairs={{0,1},{2,3},{4,5},{6,7},{8,9},{10,11},{12,13},{14,15},{16,17},{18,... | collective-permute-start | bytes 737288 | tf_op jit(solution)/shard_map/ppermute | solution.py:94
  134.2 2.8 %copy-start.4 = (f32[1,8,16,768]{3,2,1,0:T(8,128)S(1)}, f32[1,8,16,768]{3,2,1,0:T(8,128)}, u32[]{:S(2)}) copy-start(f32[1,8,16,768]{3,2,1,0:T(8,128)} %get-tuple-element.4) | copy-start | bytes 1179652
Sparse Core Ops, SparseCore 0:
  38.0 63.1 all-reduce.1
  137.2 76.1 all-gather.1

commit v11 on v10

--- a/solution.py
+++ b/solution.py
@@ -59,10 +59,13 @@
     held = lax.all_to_all(send, "tensor", split_axis=0, concat_axis=0, tiled=True)
     rows = held.reshape(tensor_count * piece, held.shape[2])
 
-    gram = lax.psum(gram_of(rows), "shard")
-    columns = gram.shape[0]
+    part = gram_of(rows)
+    columns = part.shape[0]
+    slab = jnp.zeros((8, columns), jnp.float32).at[0].set(jnp.sum(rows * rows, axis=0))
+    packed = lax.psum(jnp.concatenate([part, slab], axis=0), "shard")
+    gram = packed[:columns]
     eye = jnp.eye(columns, dtype=jnp.float32)
-    total = jnp.sum(gram * eye)
+    total = jnp.sum(packed[columns])
     denom = jnp.sqrt(total) + epsilon
     current = rows / denom
     gram = lax.optimization_barrier(gram / (denom * denom))

time: 230 us -> 229 us (level)
  no operation moved by 1% of the time
where the time goes in v11:
time: 229 us
  waiting for transfers between devices  141 us (62%)
  matrix products  27.6 us (12%)
  blocking collectives  21.9 us (10%)
  between operations  14.9 us (7%)
  local copies, waits for them, and re-layouts  10.7 us (5%)
  other arithmetic  9.75 us (4%)
  starting transfers between devices  3.38 us (1%)
    all_gather x1, waiting for transfers between devices, shards(): gathered = lax.all_gather(mine, 'tensor', axis=0, tiled=True)  75.8 us
    psum x1, waiting for transfers between devices, shards(): packed = lax.psum(jnp.concatenate([part, slab], axis=0), 'shard')  63 us
    dot_general x12, matrix products, dot(): jnp.dot(x, y, precision=PRECISION, preferred_element_type=jnp.float32)  26.3 us
    all_to_all x1, blocking collectives, shards(): lax.all_to_all(send, 'tensor', split_axis=0, concat_axis=0, tiled=True)  21.9 us
    slice x1, local copies, waits for them, and re-layouts, shards(): update_wide = gathered[:, :wide_rows]  5.94 us
  transfers between devices with their start and end apart: 3, of which 3 were waited for; matrix products, arithmetic and copies ran while one was open for 1% of the time, Pallas kernels for 0%

profile of v11, /device:TPU:1, one launch (start us, length us, event | category | flops | bytes accessed | tf_op | source)
XLA Modules:
  0.0 228.9 jit_solution(7076943141954339419)
XLA Ops:
  7.2 1.0 broadcast_multiply_fusion.1
  8.2 0.3 copy-done
  8.6 0.7 convert_add_fusion.3
  9.3 1.0 broadcast_multiply_fusion
  10.4 1.1 fusion.20
  11.5 0.1 maximum_maximum_fusion
  11.6 21.9 %all_to_all.5 = f32[16,16,768]{2,1,0:T(8,128)S(1)} all-to-all(f32[16,16,768]{2,1,0:T(8,128)S(1)} %bitcast.34), channel_id=1, replica_groups=mesh['shard'=8,'tensor'=16] {'tensor'}, dimensions={0} | all-to-all | bytes 1572864 | tf_op jit(solution)/shard_map/all_to_all | solution.py:59
  33.6 1.3 convolution_bitcast_fusion
  34.9 1.6 select_maximum_fusion
  36.5 0.2 all-gather.2.cloned.1.call-start
  36.8 63.0 %all-reduce.3.cloned.1.call-done = f32[776,768]{1,0:T(8,128)} async-done(((f32[776,768]{1,0:T(8,128)}), f32[776,768]{1,0:T(8,128)}) %all-reduce.3.cloned.1.call-update) | async-done | bytes 2383888 | tf_op jit(solution)/shard_map/psum | solution.py:65
  99.8 1.3 slice_reduce_fusion
  101.8 1.8 slice_divide_fusion
  103.7 3.3 %multiply_add_fusion.1 = f32[768,768]{1,0:T(8,128)S(1)} fusion(f32[768,768]{1,0:T(8,128)S(1)} %slice_divide_fusion), kind=kOutput, calls=%fused_computation.7 | convolution fusion | flops 2719678464 | bytes 4718592 | tf_op jit(solution)/shard_map/dot_general | solution.py:23
  107.0 3.1 %fusion.1 = f32[768,768]{1,0:T(8,128)S(1)} fusion(f32[768,768]{1,0:T(8,128)S(1)} %slice_divide_fusion, f32[768,768]{1,0:T(8,128)S(1)} %multiply_add_fusion.1), kind=kOutput, calls=%fused_computation.9 | convolution fusion | flops 2719678464 | bytes 7077888 | tf_op jit(solution)/shard_map/dot_general | solution.py:23
  110.1 3.2 %fusion = f32[768,768]{1,0:T(8,128)S(1)} fusion(f32[768,768]{1,0:T(8,128)S(1)} %fusion.1, f32[768,768]{1,0:T(8,128)S(1)} %multiply_add_fusion.1), kind=kOutput, calls=%fused_computation.8 | convolution fusion | flops 2719678464 | bytes 7077888 | tf_op jit(solution)/shard_map/dot_general | solution.py:23
  113.4 1.4 convolution_add_fusion.1
  114.8 3.5 %multiply_add_fusion = f32[768,768]{1,0:T(8,128)S(1)} fusion(f32[768,768]{1,0:T(8,128)S(1)} %fusion), kind=kOutput, calls=%fused_computation.5 | convolution fusion | flops 2719678464 | bytes 4718592 | tf_op jit(solution)/shard_map/dot_general | solution.py:23
  118.3 3.1 %fusion.3 = f32[768,768]{1,0:T(8,128)S(1)} fusion(f32[768,768]{1,0:T(8,128)S(1)} %fusion, f32[768,768]{1,0:T(8,128)S(1)} %multiply_add_fusion), kind=kOutput, calls=%fused_computation.11 | convolution fusion | flops 2719678464 | bytes 7077888 | tf_op jit(solution)/shard_map/dot_general | solution.py:23
  121.4 1.4 convolution_add_fusion
  122.8 3.2 %fusion.2 = f32[768,768]{1,0:T(8,128)S(1)} fusion(f32[768,768]{1,0:T(8,128)S(1)} %fusion.3, f32[768,768]{1,0:T(8,128)S(1)} %multiply_add_fusion), kind=kOutput, calls=%fused_computation.10 | convolution fusion | flops 2719678464 | bytes 7077888 | tf_op jit(solution)/shard_map/dot_general | solution.py:23
  126.0 0.9 fusion.21
  126.9 1.1 fusion.18
  128.0 0.9 fusion.17
  129.0 3.1 %collective-permute-start = (f32[80,768]{1,0:T(8,128)S(1)}, f32[80,768]{1,0:T(8,128)S(1)}, u32[]{:S(2)}, u32[]{:S(2)}) collective-permute-start(f32[80,768]{1,0:T(8,128)S(1)} %fusion.17), channel_id=1, source_target_pairs={{0,1},{2,3},{4,5},{6,7},{8,9},{10,11},{12,13},{14,15},{16,17},{18,... | collective-permute-start | bytes 737288 | tf_op jit(solution)/shard_map/ppermute | solution.py:97
  132.1 1.1 fusion.6
  133.4 1.8 collective-permute-done
  135.2 0.9 maximum_select_fusion
  136.1 1.0 copy.14
  137.1 75.8 %all-gather.2.cloned.1.call-done = f32[2816,768]{1,0:T(8,128)} async-done(((f32[176,768]{1,0:T(8,128)}), f32[2816,768]{1,0:T(8,128)}) %all-gather.2.cloned.1.call-update) | async-done | bytes 8650768 | tf_op jit(solution)/shard_map/all_gather | solution.py:101
  212.9 3.2 %slice.47 = f32[8,96,768]{2,1,0:T(8,128)} slice(f32[8,352,768]{2,1,0:T(8,128)} %bitcast.32), slice={[0:8], [256:352], [0:768]} | slice | bytes 4718592 | tf_op jit(solution)/shard_map/slice | solution.py:104
  216.1 5.9 %slice.48 = f32[8,256,768]{2,1,0:T(8,128)} slice(f32[8,352,768]{2,1,0:T(8,128)} %bitcast.33), slice={[0:8], [0:256], [0:768]} | slice | bytes 12582912 | tf_op jit(solution)/shard_map/slice | solution.py:103
  (14 shorter events, 0.5 us)
Async XLA Ops:
  7.2 1.3 copy-start
  7.2 92.6 %all-reduce.3.cloned.1.call-start = ((), (), s32[]{:S(2)}) async-start(), calls=%async_computation.1 | async-start | bytes 4767744 | tf_op jit(solution)/shard_map/psum | solution.py:65
  36.5 176.4 %all-gather.2.cloned.1.call-start = ((), (), s32[]{:S(2)}) async-start(), calls=%async_computation.2 | async-start | bytes 9191424 | tf_op jit(solution)/shard_map/all_gather | solution.py:101
  129.0 6.2 %collective-permute-start = (f32[80,768]{1,0:T(8,128)S(1)}, f32[80,768]{1,0:T(8,128)S(1)}, u32[]{:S(2)}, u32[]{:S(2)}) collective-permute-start(f32[80,768]{1,0:T(8,128)S(1)} %fusion.17), channel_id=1, source_target_pairs={{0,1},{2,3},{4,5},{6,7},{8,9},{10,11},{12,13},{14,15},{16,17},{18,... | collective-permute-start | bytes 737288 | tf_op jit(solution)/shard_map/ppermute | solution.py:97
Sparse Core Ops, SparseCore 0:
  36.6 63.1 all-reduce.2
  136.2 76.6 all-gather.1

commit v12 on v10

--- a/solution.py
+++ b/solution.py
@@ -62,7 +62,7 @@
     gram = lax.psum(gram_of(rows), "shard")
     columns = gram.shape[0]
     eye = jnp.eye(columns, dtype=jnp.float32)
-    total = jnp.sum(gram * eye)
+    total = jnp.sum(lax.optimization_barrier(jnp.sum(gram * eye, axis=0)))
     denom = jnp.sqrt(total) + epsilon
     current = rows / denom
     gram = lax.optimization_barrier(gram / (denom * denom))

time: 230 us -> 230 us (level)
  no operation moved by 1% of the time
where the time goes in v12:
time: 230 us; the launch traced here: 229 us
  waiting for transfers between devices  140 us (61%)
  matrix products  28.9 us (13%)
  blocking collectives  21.9 us (10%)
  between operations  15 us (7%)
  local copies, waits for them, and re-layouts  11.5 us (5%)
  other arithmetic  8.32 us (4%)
  starting transfers between devices  3.2 us (1%)
    all_gather x1, waiting for transfers between devices, shards(): gathered = lax.all_gather(mine, 'tensor', axis=0, tiled=True)  75.3 us
    psum x1, waiting for transfers between devices, shards(): gram = lax.psum(gram_of(rows), 'shard')  63.3 us
    dot_general x12, matrix products, dot(): jnp.dot(x, y, precision=PRECISION, preferred_element_type=jnp.float32)  26.2 us
    all_to_all x1, blocking collectives, shards(): lax.all_to_all(send, 'tensor', split_axis=0, concat_axis=0, tiled=True)  21.9 us
    slice x1, local copies, waits for them, and re-layouts, shards(): update_wide = gathered[:, :wide_rows]  5.94 us
  transfers between devices with their start and end apart: 3, of which 3 were waited for; matrix products, arithmetic and copies ran while one was open for 1% of the time, Pallas kernels for 0%

profile of v12, /device:TPU:1, one launch (start us, length us, event | category | flops | bytes accessed | tf_op | source)
XLA Modules:
  0.0 229.3 jit_solution(14907512171346833527)
XLA Ops:
  7.2 1.0 broadcast_multiply_fusion.1
  8.2 0.3 copy-done
  8.6 0.7 convert_add_fusion.3
  9.3 1.0 broadcast_multiply_fusion
  10.4 1.8 fusion.20
  12.2 0.1 maximum_maximum_fusion
  12.4 21.9 %all_to_all.5 = f32[16,16,768]{2,1,0:T(8,128)S(1)} all-to-all(f32[16,16,768]{2,1,0:T(8,128)S(1)} %bitcast.34), channel_id=1, replica_groups=mesh['shard'=8,'tensor'=16] {'tensor'}, dimensions={0} | all-to-all | bytes 1572864 | tf_op jit(solution)/shard_map/all_to_all | solution.py:59
  34.3 0.9 copy-done.2
  35.2 2.7 %convolution_bitcast_fusion = f32[768,768]{1,0:T(8,128)} fusion(f32[16,16,768]{2,1,0:T(8,128)S(1)} %all_to_all.5), kind=kOutput, calls=%fused_computation.10 | convolution fusion | flops 905969664 | bytes 3145728 | tf_op jit(solution)/shard_map/dot_general | solution.py:27
  37.9 63.3 %all-reduce.2.cloned.1.call-done = f32[768,768]{1,0:T(8,128)} async-done(((f32[768,768]{1,0:T(8,128)}), f32[768,768]{1,0:T(8,128)}) %all-reduce.2.cloned.1.call-update) | async-done | bytes 2359312 | tf_op jit(solution)/shard_map/psum | solution.py:62
  101.2 1.9 select_reduce_fusion
  103.1 0.6 reduce_sum.19
  104.4 0.2 broadcast_divide_fusion
  104.6 3.3 %multiply_add_fusion.1 = f32[768,768]{1,0:T(8,128)S(1)} fusion(f32[768,768]{1,0:T(8,128)S(1)} %broadcast_divide_fusion), kind=kOutput, calls=%fused_computation.3 | convolution fusion | flops 2719678464 | bytes 4718592 | tf_op jit(solution)/shard_map/dot_general | solution.py:23
  107.9 3.1 %fusion.1 = f32[768,768]{1,0:T(8,128)S(1)} fusion(f32[768,768]{1,0:T(8,128)S(1)} %broadcast_divide_fusion, f32[768,768]{1,0:T(8,128)S(1)} %multiply_add_fusion.1), kind=kOutput, calls=%fused_computation.7 | convolution fusion | flops 2719678464 | bytes 7077888 | tf_op jit(solution)/shard_map/dot_general | solution.py:23
  111.0 3.2 %fusion = f32[768,768]{1,0:T(8,128)S(1)} fusion(f32[768,768]{1,0:T(8,128)S(1)} %fusion.1, f32[768,768]{1,0:T(8,128)S(1)} %multiply_add_fusion.1), kind=kOutput, calls=%fused_computation.6 | convolution fusion | flops 2719678464 | bytes 7077888 | tf_op jit(solution)/shard_map/dot_general | solution.py:23
  114.3 1.4 convolution_add_fusion.1
  115.7 3.5 %multiply_add_fusion = f32[768,768]{1,0:T(8,128)S(1)} fusion(f32[768,768]{1,0:T(8,128)S(1)} %fusion), kind=kOutput, calls=%fused_computation.2 | convolution fusion | flops 2719678464 | bytes 4718592 | tf_op jit(solution)/shard_map/dot_general | solution.py:23
  119.2 3.1 %fusion.3 = f32[768,768]{1,0:T(8,128)S(1)} fusion(f32[768,768]{1,0:T(8,128)S(1)} %fusion, f32[768,768]{1,0:T(8,128)S(1)} %multiply_add_fusion), kind=kOutput, calls=%fused_computation.9 | convolution fusion | flops 2719678464 | bytes 7077888 | tf_op jit(solution)/shard_map/dot_general | solution.py:23
  122.3 1.4 convolution_add_fusion
  123.7 3.2 %fusion.2 = f32[768,768]{1,0:T(8,128)S(1)} fusion(f32[768,768]{1,0:T(8,128)S(1)} %fusion.3, f32[768,768]{1,0:T(8,128)S(1)} %multiply_add_fusion), kind=kOutput, calls=%fused_computation.8 | convolution fusion | flops 2719678464 | bytes 7077888 | tf_op jit(solution)/shard_map/dot_general | solution.py:23
  126.9 0.9 fusion.21
  127.8 1.1 fusion.18
  128.9 0.9 fusion.17
  129.9 3.1 %collective-permute-start = (f32[80,768]{1,0:T(8,128)S(1)}, f32[80,768]{1,0:T(8,128)S(1)}, u32[]{:S(2)}, u32[]{:S(2)}) collective-permute-start(f32[80,768]{1,0:T(8,128)S(1)} %fusion.17), channel_id=1, source_target_pairs={{0,1},{2,3},{4,5},{6,7},{8,9},{10,11},{12,13},{14,15},{16,17},{18,... | collective-permute-start | bytes 737288 | tf_op jit(solution)/shard_map/ppermute | solution.py:94
  133.0 1.1 fusion.6
  134.3 1.8 collective-permute-done
  136.1 0.9 maximum_select_fusion
  137.0 1.0 copy.14
  138.0 75.3 %all-gather.2.cloned.1.call-done = f32[2816,768]{1,0:T(8,128)} async-done(((f32[176,768]{1,0:T(8,128)}), f32[2816,768]{1,0:T(8,128)}) %all-gather.2.cloned.1.call-update) | async-done | bytes 8650768 | tf_op jit(solution)/shard_map/all_gather | solution.py:98
  213.3 3.2 %slice.23 = f32[8,96,768]{2,1,0:T(8,128)} slice(f32[8,352,768]{2,1,0:T(8,128)} %bitcast.32), slice={[0:8], [256:352], [0:768]} | slice | bytes 4718592 | tf_op jit(solution)/shard_map/slice | solution.py:101
  216.5 5.9 %slice.24 = f32[8,256,768]{2,1,0:T(8,128)} slice(f32[8,352,768]{2,1,0:T(8,128)} %bitcast.33), slice={[0:8], [0:256], [0:768]} | slice | bytes 12582912 | tf_op jit(solution)/shard_map/slice | solution.py:100
  (20 shorter events, 0.5 us)
Async XLA Ops:
  7.2 1.3 copy-start
  7.2 94.0 %all-reduce.2.cloned.1.call-start = ((), (), s32[]{:S(2)}) async-start(), calls=%async_computation.1 | async-start | bytes 4718592 | tf_op jit(solution)/shard_map/psum | solution.py:62
  34.3 0.9 copy-start.2
  37.9 175.4 %all-gather.2.cloned.1.call-start = ((), (), s32[]{:S(2)}) async-start(), calls=%async_computation.2 | async-start | bytes 9191424 | tf_op jit(solution)/shard_map/all_gather | solution.py:98
  101.2 3.2 %copy-start.1 = (f32[768,768]{1,0:T(8,128)S(1)}, f32[768,768]{1,0:T(8,128)}, u32[]{:S(2)}) copy-start(f32[768,768]{1,0:T(8,128)} %all-reduce.2.cloned.1.call-done) | copy-start | bytes 7077892
  111.0 3.2 %copy-start.3 = (f32[16,16,768]{2,1,0:T(8,128)S(1)}, f32[16,16,768]{2,1,0:T(8,128)}, u32[]{:S(2)}) copy-start(f32[16,16,768]{2,1,0:T(8,128)} %copy-done.2) | copy-start | bytes 2359300
  129.9 6.2 %collective-permute-start = (f32[80,768]{1,0:T(8,128)S(1)}, f32[80,768]{1,0:T(8,128)S(1)}, u32[]{:S(2)}, u32[]{:S(2)}) collective-permute-start(f32[80,768]{1,0:T(8,128)S(1)} %fusion.17), channel_id=1, source_target_pairs={{0,1},{2,3},{4,5},{6,7},{8,9},{10,11},{12,13},{14,15},{16,17},{18,... | collective-permute-start | bytes 737288 | tf_op jit(solution)/shard_map/ppermute | solution.py:94
  134.1 2.8 %copy-start.4 = (f32[1,8,16,768]{3,2,1,0:T(8,128)S(1)}, f32[1,8,16,768]{3,2,1,0:T(8,128)}, u32[]{:S(2)}) copy-start(f32[1,8,16,768]{3,2,1,0:T(8,128)} %get-tuple-element.4) | copy-start | bytes 1179652
Sparse Core Ops, SparseCore 0:
  38.0 63.1 all-reduce.1
  137.1 76.1 all-gather.1
